TPU v7x, 128 devices: a whole 4x4x4 slice. The times are simulated.
128 devices in a mesh: grid: 32 (over x, y, core), orb: 4 (over z).
Axes of the slice: x: 4, y: 4, z: 4, core: 2. Of those that a mesh axis runs over, the one named last changes fastest.
Arguments:
- orbital_block: float32 [128, 192, 48, 128], P('orb', 'grid'), may hold values from -30 to 30
- potential: float32 [192, 48, 128], P('grid'), may hold values from -6 to -0.5
Outputs:
- orbitals: float32 [128, 192, 48, 128], P('orb', 'grid')
- triangle: float32 [128, 128], replicated
All inputs are finite; a program needn't handle non-finite values.
Results may differ from a plain program's by a relative error of at most 0.0003.
Values sent between devices are 32-bit elements; how exact they have to be, the bound alone decides.
No kernel may reach another device: no remote copies, remote signals or barrier semaphores. Data moves between devices by JAX's collectives and lax.ppermute only.
A program may use at most 128 MiB of HBM per device.

v0:
```python
import jax
import jax.numpy as jnp
from jax import lax
from jax.sharding import PartitionSpec as P

coefs = (
    -5369.0 / 1800.0,
    12.0 / 7.0,
    -15.0 / 56.0,
    10.0 / 189.0,
    -1.0 / 112.0,
    2.0 / 1925.0,
    -1.0 / 16632.0,
)
centre = 23.5
radius = 19.5
highest = lax.Precision.HIGHEST


def padded_2(value, sides, width):
    for axis, dim in sides:
        size, length = (lax.axis_size(axis), value.shape[dim])
        up = [(i, (i + 1) % size) for i in range(size - 1)]
        down = [(j, i) for i, j in up]
        last = lax.slice_in_dim(value, length - width, length, axis=dim)
        first = lax.slice_in_dim(value, 0, width, axis=dim)
        before = lax.ppermute(last, axis, up)
        after = lax.ppermute(first, axis, down)
        value = jnp.concatenate([before, value, after], axis=dim)
    return value


def hamiltonian(orbital_field, potential):
    slab_cells = orbital_field.shape[1]
    across = orbital_field.shape[2]
    depth_cells = orbital_field.shape[3]
    widened = padded_2(orbital_field, (("grid", 1),), 6)
    padded = jnp.pad(orbital_field, ((0, 0), (0, 0), (6, 6), (6, 6)))
    total = 3.0 * coefs[0] * orbital_field
    for k in range(1, 7):
        total = total + coefs[k] * (
            widened[:, 6 + k : 6 + k + slab_cells] + widened[:, 6 - k : 6 - k + slab_cells]
        )
        total = total + coefs[k] * (
            padded[:, :, 6 + k : 6 + k + across, 6 : 6 + depth_cells]
            + padded[:, :, 6 - k : 6 - k + across, 6 : 6 + depth_cells]
        )
        total = total + coefs[k] * (
            padded[:, :, 6 : 6 + across, 6 + k : 6 + k + depth_cells]
            + padded[:, :, 6 : 6 + across, 6 - k : 6 - k + depth_cells]
        )
    return -2.0 * total + potential[None] * orbital_field


def gram_matrix(left_rows, right_rows):
    return lax.dot_general(
        left_rows,
        right_rows,
        (((1,), (1,)), ((), ())),
        precision=highest,
        preferred_element_type=jnp.float32,
    )


def apply_rows(inverse, source_rows):
    return lax.dot_general(
        inverse,
        source_rows,
        (((0,), (0,)), ((), ())),
        precision=highest,
        preferred_element_type=jnp.float32,
    )


def cholesky_upper(matrix):
    extent = matrix.shape[0]
    positions = lax.broadcasted_iota(jnp.int32, (extent,), 0)

    def column_step(column, carry):
        remaining, upper_part = carry
        selector = (positions == column).astype(jnp.float32)
        current = jnp.sum(remaining * selector[:, None], axis=0)
        pivot_value = jnp.sum(current * selector)
        scaled = jnp.where(positions >= column, current, jnp.float32(0.0)) / jnp.sqrt(pivot_value)
        upper_part = upper_part + selector[:, None] * scaled[None, :]
        remaining = remaining - scaled[:, None] * scaled[None, :]
        return (remaining, upper_part)

    start = (matrix, jnp.zeros((extent, extent), jnp.float32))
    return lax.fori_loop(0, extent, column_step, start)[1]


def upper_inverse(triangle):
    extent = triangle.shape[0]
    positions = lax.broadcasted_iota(jnp.int32, (extent,), 0)

    def back_step(turn, inverse):
        column = extent - 1 - turn
        selector = (positions == column).astype(jnp.float32)
        tri_row = jnp.sum(triangle * selector[:, None], axis=0)
        diag_value = jnp.sum(tri_row * selector)
        carried = jnp.dot(tri_row, inverse, precision=highest, preferred_element_type=jnp.float32)
        new_row = (selector - carried) / diag_value
        return inverse + selector[:, None] * new_row[None, :]

    return lax.fori_loop(0, extent, back_step, jnp.zeros((extent, extent), jnp.float32))


def factorize(rows_block, lead_sum, trail_sum, inv_cells):
    panel_rows = rows_block.shape[0] // 2
    leading = lead_sum(gram_matrix(rows_block[:panel_rows], rows_block)) * inv_cells
    first_r = cholesky_upper(leading[:, :panel_rows])
    first_inverse = upper_inverse(first_r)
    coupling = apply_rows(first_inverse, leading[:, panel_rows:])
    first_q = apply_rows(first_inverse, rows_block[:panel_rows])
    remainder = rows_block[panel_rows:] - apply_rows(coupling, first_q)
    trailing = trail_sum(gram_matrix(remainder, remainder)) * inv_cells
    second_r = cholesky_upper(trailing)
    upper_rows = jnp.concatenate([first_r, coupling], axis=1)
    lower_rows = jnp.concatenate(
        [jnp.zeros((second_r.shape[0], panel_rows), jnp.float32), second_r], axis=1
    )
    return jnp.concatenate([upper_rows, lower_rows], axis=0)


def local(orbital_block, potential):
    orb_rows = orbital_block.shape[0]
    first = (hamiltonian(orbital_block, potential) - centre * orbital_block) / radius
    filtered = 2.0 * (hamiltonian(first, potential) - centre * first) / radius - orbital_block
    filtered = filtered.reshape(orb_rows, -1)
    inv_cells = 1.0 / (lax.axis_size("grid") * filtered.shape[1])
    gathered = lax.all_gather(filtered, "orb", axis=0, tiled=True)

    def lead_sum(term):
        return lax.psum(term, "grid")

    def trail_sum(term):
        return lax.psum(term, "grid")

    triangle = factorize(gathered, lead_sum, trail_sum, inv_cells)
    inverse = upper_inverse(triangle)
    own_columns = lax.dynamic_slice_in_dim(inverse, lax.axis_index("orb") * orb_rows, orb_rows, 1)
    orbitals = apply_rows(own_columns, gathered)
    return (orbitals.reshape(orbital_block.shape), triangle)


def solution(mesh):
    in_specs = (P("orb", "grid", None, None), P("grid", None, None))
    out_specs = (P("orb", "grid", None, None), P())
    return jax.shard_map(local, mesh=mesh, in_specs=in_specs, out_specs=out_specs, check_vma=False)
```

profile of v0, /device:TPU:0, one launch (start us, length us, event | category | flops | bytes accessed | tf_op | source)
XLA Modules:
  0.0 1270.5 jit_solution(10992658229111029657)
XLA Ops:
  7.2 1.9 collective-permute-start.1
  9.1 1.3 collective-permute-start
  10.4 6.1 collective-permute-done.1
  16.5 2.2 copy-done.3
  19.1 3.0 constant_dynamic-update-slice_fusion.1
  22.1 2.2 copy-done.4
  24.3 3.0 constant_dynamic-update-slice_fusion
  27.3 1.1 copy-done.1
  28.5 26.3 %broadcast_multiply_fusion = (f32[32,6,48,128]{3,2,1,0:T(8,128)}, f32[32,6,48,128]{3,2,1,0:T(8,128)}) fusion(f32[32,6,48,128]{3,2,1,0:T(8,128)S(1)} %copy-done.2, f32[6,48,128]{2,1,0:T(8,128)S(1)} %copy-done.6, f32[32,6,48,128]{3,2,1,0:T(8,128)} %copy-done.4, f32[32,6,48,128]{3,2,1,0:T(8,128)} %copy-done.3, f32[32,12,48,128]{3,2,1,0:T(8,128)} %copy-done.1, ...), kind=kLoop, calls=%fused_computation.235 | loop fusion | flops 71958528 | bytes 70926336 | tf_op jit(solution)/shard_map/div | solution.py:128
  54.8 1.3 collective-permute-start.2
  56.1 50.8 %collective-permute-start.3 = (f32[32,6,48,128]{3,2,1,0:T(8,128)}, f32[32,6,48,128]{3,2,1,0:T(8,128)}, u32[]{:S(2)}, u32[]{:S(2)}) collective-permute-start(f32[32,6,48,128]{3,2,1,0:T(8,128)} %get-tuple-element.432), channel_id=1, source_target_pairs={{0,4},{4,8},{8,12},{12,16},{16,20},{20,24},{24,28},{28,32},{32,36}... | collective-permute-start | bytes 14155784 | tf_op jit(solution)/shard_map/ppermute | solution.py:27
  106.8 3.6 collective-permute-done.2
  110.5 2.1 collective-permute-done.3
  112.5 83.2 %multiply_subtract_fusion.2 = f32[32,6,48,128]{3,2,1,0:T(8,128)} fusion(f32[32,6,48,128]{3,2,1,0:T(8,128)} %param.10, f32[32,6,48,128]{3,2,1,0:T(8,128)} %get-tuple-element.433, f32[32,6,48,128]{3,2,1,0:T(8,128)} %get-tuple-element.432, f32[32,6,48,128]{3,2,1,0:T(8,128)} %collective-permute-done.2, f32[32,6,48,128]{3,2,1,0:T(8,128)} %collective-permute-done.3, ...), kind=kLoop, calls=%fused_computation.233 | loop fusion | flops 84934656 | bytes 28459008 | tf_op jit(solution)/shard_map/sub | solution.py:129
  195.7 7.3 copy.7
  203.0 223.4 %all-gather.2.cloned.1.call-done = f32[128,36864]{1,0:T(8,128)} async-done(((f32[32,36864]{1,0:T(8,128)}), f32[128,36864]{1,0:T(8,128)}) %all-gather.2.cloned.1.call-update) | async-done | bytes 18874384 | tf_op jit(solution)/shard_map/all_gather | solution.py:132
  426.4 23.6 %fusion.30 = f32[64,128]{1,0:T(8,128)S(1)} fusion(f32[128,36864]{1,0:T(8,128)} %all-gather.2.cloned.1.call-done), kind=kOutput, calls=%fused_computation.113 | convolution fusion | flops 3623878656 | bytes 28344320 | tf_op jit(solution)/shard_map/dot_general | solution.py:56
  450.1 128.1 %psum.14 = f32[64,128]{1,0:T(8,128)S(1)} all-reduce(f32[64,128]{1,0:T(8,128)S(1)} %fusion.30), channel_id=1, replica_groups=mesh['grid'=32,'orb'=4] {'grid'}, use_global_device_ids=true, to_apply=%region_0.1 | all-reduce | flops 8192 | bytes 65536 | tf_op jit(solution)/shard_map/psum | solution.py:135
  578.2 97.9 %while.64 = (s32[]{:T(128)}, f32[64,64]{1,0:T(8,128)S(1)}, f32[64,64]{1,0:T(8,128)S(1)}, s32[]{:T(128)}, s32[]{:T(128)}) while((s32[]{:T(128)}, f32[64,64]{1,0:T(8,128)S(1)}, f32[64,64]{1,0:T(8,128)S(1)}, s32[]{:T(128)}, s32[]{:T(128)}) %tuple.131), condition=%wide.region_4.5_spmd.clone.clone, body=%wide.region_1.4_spmd.clone.clone.sunk | while | flops 29122 | bytes 84067 | solution.py:90
  676.0 101.2 %while.62 = (s32[]{:T(128)}, f32[64,64]{1,0:T(8,128)S(1)}, f32[64,64]{1,0:T(8,128)S(1)}, s32[]{:T(128)}, s32[]{:T(128)}, /*index=5*/s32[]{:T(128)}) while((s32[]{:T(128)}, f32[64,64]{1,0:T(8,128)S(1)}, f32[64,64]{1,0:T(8,128)S(1)}, s32[]{:T(128)}, s32[]{:T(128)}, /*index=5*/s32[]{:T(128)}) %tuple.134), condition=%wide.region_8.9_spmd.clone, body=%wide.region_5.8_spmd.clone.sunk | while | flops 74243 | bytes 67696 | solution.py:106
  777.5 13.0 %fusion.28 = f32[64,36864]{1,0:T(8,128)} fusion(f32[64,64]{1,0:T(8,128)S(1)} %get-tuple-element.325, f32[128,36864]{1,0:T(8,128)} %all-gather.2.cloned.1.call-done), kind=kOutput, calls=%fused_computation.111 | convolution fusion | flops 1811939328 | bytes 18890752 | tf_op jit(solution)/shard_map/dot_general | solution.py:66
  790.5 13.3 %convolution_subtract_fusion = f32[64,36864]{1,0:T(8,128)} fusion(f32[64,64]{1,0:T(8,128)S(1)} %fusion.143, f32[64,36864]{1,0:T(8,128)} %fusion.28, f32[128,36864]{1,0:T(8,128)S(1)} %copy-done), kind=kOutput, calls=%fused_computation.94 | convolution fusion | flops 1814298624 | bytes 28327936 | tf_op jit(solution)/shard_map/dot_general | solution.py:66
  803.8 11.6 fusion.146
  815.3 123.8 %psum.15 = f32[64,64]{1,0:T(8,128)S(1)} all-reduce(f32[64,64]{1,0:T(8,128)S(1)} %fusion.146), channel_id=1, replica_groups=mesh['grid'=32,'orb'=4] {'grid'}, use_global_device_ids=true, to_apply=%region_9.10 | all-reduce | flops 4096 | bytes 32768 | tf_op jit(solution)/shard_map/psum | solution.py:138
  939.1 97.8 %while.65 = (s32[]{:T(128)}, f32[64,64]{1,0:T(8,128)S(1)}, f32[64,64]{1,0:T(8,128)S(1)}, s32[]{:T(128)}, s32[]{:T(128)}) while((s32[]{:T(128)}, f32[64,64]{1,0:T(8,128)S(1)}, f32[64,64]{1,0:T(8,128)S(1)}, s32[]{:T(128)}, s32[]{:T(128)}) %tuple.137), condition=%wide.region_13.14_spmd.clone.clone, body=%wide.region_10.13_spmd.clone.clone.sunk | while | flops 29122 | bytes 84067 | solution.py:90
  1037.0 210.7 %while.63 = (s32[]{:T(128)}, f32[128,128]{1,0:T(8,128)S(1)}, f32[128,128]{1,0:T(8,128)S(1)}, s32[]{:T(128)}, s32[]{:T(128)}, /*index=5*/s32[]{:T(128)}) while((s32[]{:T(128)}, f32[128,128]{1,0:T(8,128)S(1)}, f32[128,128]{1,0:T(8,128)S(1)}, s32[]{:T(128)}, s32[]{:T(128)}, /*index=5*/s32[]{:T(128)}) %tuple.140), condition=%wide.region_17.18_spmd.clone, body=%wide.region_14.17_spmd.clone.sunk | while | flops 295939 | bytes 266352 | solution.py:106
  1037.8 0.8 fusion.174
  1044.4 0.8 fusion.174
  1046.0 0.8 fusion.174
  1052.6 0.8 fusion.174
  1247.8 12.8 %convolution_bitcast_fusion.2 = f32[4,8,288,128]{3,1,2,0:T(8,128)S(1)} fusion(f32[128,36864]{1,0:T(8,128)} %all-gather.2.cloned.1.call-done, f32[128,128]{1,0:T(8,128)S(1)} %get-tuple-element.327, s32[]{:T(128)S(6)} %select_n.38), kind=kOutput, calls=%fused_computation.236 | convolution fusion | flops 1811939328 | bytes 23658500 | tf_op jit(solution)/shard_map/dot_general | solution.py:66
  1260.6 3.0 copy.5
  (1621 shorter events, 406.1 us)
Async XLA Ops:
  7.2 419.3 %all-gather.2.cloned.1.call-start = ((), (), s32[]{:S(2)}) async-start(), calls=%async_computation | async-start | bytes 23592960 | tf_op jit(solution)/shard_map/all_gather | solution.py:132
  7.2 11.9 copy-start.2
  7.2 9.3 collective-permute-start.1
  9.1 13.0 %collective-permute-start = (f32[32,6,48,128]{3,2,1,0:T(8,128)}, f32[32,6,48,128]{3,2,1,0:T(8,128)S(1)}, u32[]{:S(2)}, u32[]{:S(2)}) collective-permute-start(f32[32,6,48,128]{3,2,1,0:T(8,128)} %param.10), channel_id=1, source_target_pairs={{4,0},{8,4},{12,8},{16,12},{20,16},{24,20},{28,24},{32,28},{36,32}... | collective-permute-start | bytes 14155784 | tf_op jit(solution)/shard_map/ppermute | solution.py:28
  16.5 2.2 copy-start.3
  22.1 6.4 copy-start.1
  22.1 2.2 copy-start.4
  24.3 4.2 copy-start.6
  54.8 55.7 %collective-permute-start.2 = (f32[32,6,48,128]{3,2,1,0:T(8,128)}, f32[32,6,48,128]{3,2,1,0:T(8,128)}, u32[]{:S(2)}, u32[]{:S(2)}) collective-permute-start(f32[32,6,48,128]{3,2,1,0:T(8,128)} %get-tuple-element.432), channel_id=1, source_target_pairs={{4,0},{8,4},{12,8},{16,12},{20,16},{24,20},{28,24},{32,28},{36,32}... | collective-permute-start | bytes 14155784 | tf_op jit(solution)/shard_map/ppermute | solution.py:28
  56.1 56.5 %collective-permute-start.3 = (f32[32,6,48,128]{3,2,1,0:T(8,128)}, f32[32,6,48,128]{3,2,1,0:T(8,128)}, u32[]{:S(2)}, u32[]{:S(2)}) collective-permute-start(f32[32,6,48,128]{3,2,1,0:T(8,128)} %get-tuple-element.432), channel_id=1, source_target_pairs={{0,4},{4,8},{8,12},{12,16},{16,20},{20,24},{24,28},{28,32},{32,36}... | collective-permute-start | bytes 14155784 | tf_op jit(solution)/shard_map/ppermute | solution.py:27
  777.5 13.0 %copy-start = (f32[128,36864]{1,0:T(8,128)S(1)}, f32[128,36864]{1,0:T(8,128)}, u32[]{:S(2)}) copy-start(f32[128,36864]{1,0:T(8,128)} %all-gather.2.cloned.1.call-done) | copy-start | bytes 56623108
  1247.8 12.9 %copy-start.5 = (f32[128,128]{1,0:T(8,128)}, f32[128,128]{1,0:T(8,128)S(1)}, u32[]{:S(2)}) copy-start(f32[128,128]{1,0:T(8,128)S(1)} %get-tuple-element.601) | copy-start | bytes 196612
Sparse Core Ops, SparseCore 0:
  203.1 223.2 all-gather.1
where the time goes:
time: 1280 us; the launch traced here: 1270 us
  other arithmetic  366 us (29%)
  blocking collectives  252 us (20%)
  waiting for transfers between devices  235 us (18%)
  matrix products  227 us (18%)
  loops' own time  99.1 us (8%)
  starting transfers between devices  55.2 us (4%)
  local copies, waits for them, and re-layouts  22.2 us (2%)
  between operations  14.2 us (1%)
    all_gather x1, waiting for transfers between devices, local(): gathered = lax.all_gather(filtered, 'orb', axis=0, tiled=True)  223 us
    dot_general x192, matrix products, back_step(): jnp.dot(tri_row, inverse, precision=highest, preferred_element_type=jnp.f...  152 us
    psum x1, blocking collectives, lead_sum(): return lax.psum(term, 'grid')  128 us
    psum x1, blocking collectives, trail_sum(): return lax.psum(term, 'grid')  124 us
    reduce_sum x192, other arithmetic, back_step(): diag_value = jnp.sum(tri_row * selector)  117 us
    another operation x2, loops' own time, cholesky_upper(): return lax.fori_loop(0, extent, column_step, start)[1]  94.2 us
    sub x1, other arithmetic, local(): 2.0 * (hamiltonian(first, potential) - centre * first) / radius  83.2 us
    reduce_sum x128, other arithmetic, column_step(): pivot_value = jnp.sum(current * selector)  77.3 us
  transfers between devices with their start and end apart: 5, of which 4 were waited for; matrix products, arithmetic and copies ran while one was open for 0% of the time, Pallas kernels for 0%

commit v1 on v0

v1 whole, which is shorter than its diff:
```python
import jax
import jax.numpy as jnp
from jax import lax
from jax.experimental import pallas as pl
from jax.experimental.pallas import tpu as pltpu
from jax.sharding import PartitionSpec as P

coefs = (
    -5369.0 / 1800.0,
    12.0 / 7.0,
    -15.0 / 56.0,
    10.0 / 189.0,
    -1.0 / 112.0,
    2.0 / 1925.0,
    -1.0 / 16632.0,
)
centre = 23.5
radius = 19.5
highest = lax.Precision.HIGHEST


def padded_2(value, sides, width):
    for axis, dim in sides:
        size, length = (lax.axis_size(axis), value.shape[dim])
        up = [(i, (i + 1) % size) for i in range(size - 1)]
        down = [(j, i) for i, j in up]
        last = lax.slice_in_dim(value, length - width, length, axis=dim)
        first = lax.slice_in_dim(value, 0, width, axis=dim)
        before = lax.ppermute(last, axis, up)
        after = lax.ppermute(first, axis, down)
        value = jnp.concatenate([before, value, after], axis=dim)
    return value


def hamiltonian(orbital_field, potential):
    slab_cells = orbital_field.shape[1]
    across = orbital_field.shape[2]
    depth_cells = orbital_field.shape[3]
    widened = padded_2(orbital_field, (("grid", 1),), 6)
    padded = jnp.pad(orbital_field, ((0, 0), (0, 0), (6, 6), (6, 6)))
    total = 3.0 * coefs[0] * orbital_field
    for k in range(1, 7):
        total = total + coefs[k] * (
            widened[:, 6 + k : 6 + k + slab_cells] + widened[:, 6 - k : 6 - k + slab_cells]
        )
        total = total + coefs[k] * (
            padded[:, :, 6 + k : 6 + k + across, 6 : 6 + depth_cells]
            + padded[:, :, 6 - k : 6 - k + across, 6 : 6 + depth_cells]
        )
        total = total + coefs[k] * (
            padded[:, :, 6 : 6 + across, 6 + k : 6 + k + depth_cells]
            + padded[:, :, 6 : 6 + across, 6 - k : 6 - k + depth_cells]
        )
    return -2.0 * total + potential[None] * orbital_field


def gram_matrix(left_rows, right_rows):
    return lax.dot_general(
        left_rows,
        right_rows,
        (((1,), (1,)), ((), ())),
        precision=highest,
        preferred_element_type=jnp.float32,
    )


def apply_rows(inverse, source_rows):
    return lax.dot_general(
        inverse,
        source_rows,
        (((0,), (0,)), ((), ())),
        precision=highest,
        preferred_element_type=jnp.float32,
    )


def mix_rows(weights, source_rows):
    return lax.dot_general(
        weights,
        source_rows,
        (((1,), (0,)), ((), ())),
        precision=highest,
        preferred_element_type=jnp.float32,
    )


def exchange_sum(value, axis):
    size = lax.axis_size(axis)
    if size & (size - 1):
        return lax.psum(value, axis)
    step = 1
    while step < size:
        pairs = [(i, i ^ step) for i in range(size)]
        value = value + lax.ppermute(value, axis, pairs)
        step *= 2
    return value


def eliminate_kernel(source_ref, result_ref):
    result_ref[...] = source_ref[...]
    rows, width = result_ref.shape
    lanes = lax.broadcasted_iota(jnp.int32, (1, width), 1)
    cols = lax.broadcasted_iota(jnp.int32, (rows, width), 1)
    row_ids = lax.broadcasted_iota(jnp.int32, (rows, 1), 0)

    def column_step(column, carry):
        current = result_ref[pl.ds(column, 1), :]
        pivot_value = jnp.sum(jnp.where(lanes == column, current, 0.0), axis=1, keepdims=True)
        root = jnp.sqrt(pivot_value)
        scaled = jnp.where(lanes >= column, current, 0.0) / root
        whole = result_ref[...]
        below = jnp.sum(jnp.where(cols == column, whole, 0.0), axis=1, keepdims=True) / root
        below = jnp.where(row_ids > column, below, 0.0)
        whole = whole - below * scaled
        result_ref[...] = jnp.where(row_ids == column, scaled, whole)
        return carry

    lax.fori_loop(0, rows, column_step, 0)


def eliminate(matrix, extra):
    source = jnp.concatenate([matrix, extra], axis=1)
    return pl.pallas_call(
        eliminate_kernel,
        out_shape=jax.ShapeDtypeStruct(source.shape, jnp.float32),
    )(source)


def factorize(rows_block, inv_cells):
    panel_rows = rows_block.shape[0] // 2
    leading = exchange_sum(gram_matrix(rows_block[:panel_rows], rows_block), "grid") * inv_cells
    eye = jnp.eye(panel_rows, dtype=jnp.float32)
    first = eliminate(leading, eye)
    first_r = first[:, :panel_rows]
    coupling = first[:, panel_rows : 2 * panel_rows]
    first_lower_inv = first[:, 2 * panel_rows :]
    first_q = mix_rows(first_lower_inv, rows_block[:panel_rows])
    remainder = rows_block[panel_rows:] - apply_rows(coupling, first_q)
    trailing = exchange_sum(gram_matrix(remainder, remainder), "grid") * inv_cells
    second = eliminate(trailing, eye)
    second_r = second[:, :panel_rows]
    second_lower_inv = second[:, panel_rows:]
    upper_rows = jnp.concatenate([first_r, coupling], axis=1)
    lower_rows = jnp.concatenate(
        [jnp.zeros((second_r.shape[0], panel_rows), jnp.float32), second_r], axis=1
    )
    triangle = jnp.concatenate([upper_rows, lower_rows], axis=0)
    return triangle, first_q, second_lower_inv, remainder


def local(orbital_block, potential):
    orb_rows = orbital_block.shape[0]
    first = (hamiltonian(orbital_block, potential) - centre * orbital_block) / radius
    filtered = 2.0 * (hamiltonian(first, potential) - centre * first) / radius - orbital_block
    filtered = filtered.reshape(orb_rows, -1)
    inv_cells = 1.0 / (lax.axis_size("grid") * filtered.shape[1])
    gathered = lax.all_gather(filtered, "orb", axis=0, tiled=True)
    triangle, first_q, second_lower_inv, remainder = factorize(gathered, inv_cells)
    second_q = mix_rows(second_lower_inv, remainder)
    orbitals = jnp.concatenate([first_q, second_q], axis=0)
    orbitals = lax.dynamic_slice_in_dim(orbitals, lax.axis_index("orb") * orb_rows, orb_rows, 0)
    return (orbitals.reshape(orbital_block.shape), triangle)


def solution(mesh):
    in_specs = (P("orb", "grid", None, None), P("grid", None, None))
    out_specs = (P("orb", "grid", None, None), P())
    return jax.shard_map(local, mesh=mesh, in_specs=in_specs, out_specs=out_specs, check_vma=False)
```

time: 1280 us -> 569 us (0.44)
  other arithmetic: 366 us -> 112 us
  blocking collectives: 252 us -> 0 us
  matrix products: 227 us -> 69 us
  loops' own time: 99.1 us -> 0 us
  waiting for transfers between devices: 235 us -> 256 us
  starting transfers between devices: 55.2 us -> 74.3 us
  Pallas kernels: 0 us -> 16.6 us
    psum x2 -> x0, blocking collectives: 252 us -> none  [the longest x1 128 us: lead_sum(): return lax.psum(term, 'grid')]
    reduce_sum x640 -> x0, other arithmetic: 224 us -> none  [the longest x192 117 us: back_step(): diag_value = jnp.sum(tri_row * selector)]
    dot_general x192 -> x2, matrix products: 152 us -> 22.7 us  [mix_rows(): lax.dot_general(weights, source_rows, (((1,), (0,)), ((), ())), precision...]
    another operation x4 -> x0, loops' own time: 99.1 us -> none  [the longest x2 94.2 us: cholesky_upper(): return lax.fori_loop(0, extent, column_step, start)[1]]
    add x320 -> x8, other arithmetic: 29.4 us -> 0.04 us  [exchange_sum(): value = value + lax.ppermute(value, axis, pairs)]
    dot_general x4 -> x1, matrix products: 39.3 us -> 15.3 us  [apply_rows(): lax.dot_general(inverse, source_rows, (((0,), (0,)), ((), ())), precision...]
    ppermute x0 -> x10, waiting for transfers between devices: none -> 21.5 us  [exchange_sum(): value = value + lax.ppermute(value, axis, pairs)]
    ppermute x0 -> x10, starting transfers between devices: none -> 18.5 us  [exchange_sum(): value = value + lax.ppermute(value, axis, pairs)]
  transfers between devices with their start and end apart: 5 -> 15, of which waited for: 4 -> 14; matrix products, arithmetic and copies ran while one was open for 0% -> 1% of each run, Pallas kernels for 0% -> 0%
where the time goes in v1:
time: 569 us; the launch traced here: 565 us
  waiting for transfers between devices  256 us (45%)
  other arithmetic  112 us (20%)
  starting transfers between devices  74.3 us (13%)
  matrix products  69 us (12%)
  local copies, waits for them, and re-layouts  22.2 us (4%)
  Pallas kernels  16.6 us (3%)
  between operations  14.5 us (3%)
    all_gather x1, waiting for transfers between devices, local(): gathered = lax.all_gather(filtered, 'orb', axis=0, tiled=True)  223 us
    sub x1, other arithmetic, local(): 2.0 * (hamiltonian(first, potential) - centre * first) / radius  82.7 us
    ppermute x2, starting transfers between devices, padded_2(): before = lax.ppermute(last, axis, up)  53.1 us
    dot_general x2, matrix products, gram_matrix(): lax.dot_general(left_rows, right_rows, (((1,), (1,)), ((), ())), precisio...  31.1 us
    div x1, other arithmetic, local(): (hamiltonian(orbital_block, potential) - centre * orbital_block) / radius  26.4 us
    dot_general x2, matrix products, mix_rows(): lax.dot_general(weights, source_rows, (((1,), (0,)), ((), ())), precision...  22.7 us
    ppermute x10, waiting for transfers between devices, exchange_sum(): value = value + lax.ppermute(value, axis, pairs)  21.5 us
    unnamed x28, local copies, waits for them, and re-layouts  19.2 us
  transfers between devices with their start and end apart: 15, of which 14 were waited for; matrix products, arithmetic and copies ran while one was open for 1% of the time, Pallas kernels for 0%

profile of v1, /device:TPU:0, one launch (start us, length us, event | category | flops | bytes accessed | tf_op | source)
XLA Modules:
  0.0 565.0 jit_solution(16473589860159643761)
XLA Ops:
  10.4 6.1 %collective-permute-done.1 = f32[32,6,48,128]{3,2,1,0:T(8,128)S(1)} collective-permute-done((f32[32,6,48,128]{3,2,1,0:T(8,128)}, f32[32,6,48,128]{3,2,1,0:T(8,128)S(1)}, u32[]{:S(2)}, u32[]{:S(2)}) %collective-permute-start.1) | collective-permute-done | bytes 4718624 | tf_op jit(solution)/shard_map/ppermute | solution.py:29
  16.5 2.2 copy-done.4
  19.0 3.0 constant_dynamic-update-slice_fusion.1
  22.0 2.2 copy-done.5
  24.2 3.0 constant_dynamic-update-slice_fusion
  28.4 26.4 %broadcast_multiply_fusion = (f32[32,6,48,128]{3,2,1,0:T(8,128)}, f32[32,6,48,128]{3,2,1,0:T(8,128)}) fusion(f32[32,6,48,128]{3,2,1,0:T(8,128)S(1)} %copy-done.3, f32[6,48,128]{2,1,0:T(8,128)S(1)} %copy-done.6, f32[32,6,48,128]{3,2,1,0:T(8,128)} %copy-done.5, f32[32,6,48,128]{3,2,1,0:T(8,128)} %copy-done.4, f32[32,12,48,128]{3,2,1,0:T(8,128)} %copy-done.1, ...), kind=kLoop, calls=%fused_computation.193 | loop fusion | flops 71958528 | bytes 70926336 | tf_op jit(solution)/shard_map/div | solution.py:153
  56.1 51.3 %collective-permute-start.3 = (f32[32,6,48,128]{3,2,1,0:T(8,128)}, f32[32,6,48,128]{3,2,1,0:T(8,128)}, u32[]{:S(2)}, u32[]{:S(2)}) collective-permute-start(f32[32,6,48,128]{3,2,1,0:T(8,128)} %get-tuple-element.2), channel_id=1, source_target_pairs={{0,4},{4,8},{8,12},{12,16},{16,20},{20,24},{24,28},{28,32},{32,36}... | collective-permute-start | bytes 14155784 | tf_op jit(solution)/shard_map/ppermute | solution.py:29
  107.5 3.1 collective-permute-done.2
  110.6 2.1 collective-permute-done.3
  112.6 82.7 %multiply_subtract_fusion = f32[32,6,48,128]{3,2,1,0:T(8,128)} fusion(f32[32,6,48,128]{3,2,1,0:T(8,128)} %param.2, f32[32,6,48,128]{3,2,1,0:T(8,128)} %get-tuple-element.3, f32[32,6,48,128]{3,2,1,0:T(8,128)} %get-tuple-element.2, f32[32,6,48,128]{3,2,1,0:T(8,128)} %collective-permute-done.2, f32[32,6,48,128]{3,2,1,0:T(8,128)} %collective-permute-done.3, ...), kind=kLoop, calls=%fused_computation.191 | loop fusion | flops 84934656 | bytes 28459008 | tf_op jit(solution)/shard_map/sub | solution.py:154
  195.3 7.3 %copy.7 = f32[4,8,288,128]{3,1,2,0:T(8,128)} copy(f32[4,8,288,128]{3,2,1,0:T(8,128)} %bitcast.18) | data formatting | bytes 9437184
  202.6 223.4 %all-gather.2.cloned.1.call-done = f32[128,36864]{1,0:T(8,128)} async-done(((f32[32,36864]{1,0:T(8,128)}), f32[128,36864]{1,0:T(8,128)}) %all-gather.2.cloned.1.call-update) | async-done | bytes 18874384 | tf_op jit(solution)/shard_map/all_gather | solution.py:157
  426.1 23.6 %fusion.2 = f32[64,128]{1,0:T(8,128)S(1)} fusion(f32[128,36864]{1,0:T(8,128)} %all-gather.2.cloned.1.call-done), kind=kOutput, calls=%fused_computation.69 | convolution fusion | flops 3623878656 | bytes 28344320 | tf_op jit(solution)/shard_map/dot_general | solution.py:58
  452.5 2.4 collective-permute-done.5
  454.9 3.0 collective-permute-start.6
  457.9 2.4 collective-permute-done.6
  462.0 2.4 collective-permute-done.7
  464.4 3.1 collective-permute-start.8
  467.5 2.4 collective-permute-done.8
  470.5 8.4 %shard_map.41 = f32[64,192]{1,0:T(8,128)} custom-call(f32[64,192]{1,0:T(8,128)} %pad_maximum_fusion.2.source_ref), custom_call_target="tpu_custom_call" | custom-call | tf_op jit(solution)/shard_map/pallas_call | solution.py:123
  478.8 11.3 %fusion = f32[64,36864]{1,0:T(8,128)S(1)} fusion(f32[128,36864]{1,0:T(8,128)} %all-gather.2.cloned.1.call-done, f32[64,192]{1,0:T(8,128)} %shard_map.41), kind=kOutput, calls=%fused_computation.67 | convolution fusion | flops 1811939328 | bytes 18907136 | tf_op jit(solution)/shard_map/dot_general | solution.py:78
  490.2 15.3 %convolution_subtract_fusion = f32[64,36864]{1,0:T(8,128)S(1)} fusion(f32[64,36864]{1,0:T(8,128)S(1)} %fusion, f32[128,36864]{1,0:T(8,128)} %all-gather.2.cloned.1.call-done, f32[64,192]{1,0:T(8,128)S(1)} %copy-done.7), kind=kOutput, calls=%fused_computation.48 | convolution fusion | flops 1814298624 | bytes 28344320 | tf_op jit(solution)/shard_map/dot_general | solution.py:68
  505.5 7.4 %fusion.121 = f32[64,64]{1,0:T(8,128)S(1)} fusion(f32[64,36864]{1,0:T(8,128)S(1)} %convolution_subtract_fusion), kind=kOutput, calls=%fused_computation.211 | convolution fusion | flops 1811939328 | bytes 9453568 | tf_op jit(solution)/shard_map/dot_general | solution.py:58
  515.7 2.4 collective-permute-done.10
  518.1 3.0 collective-permute-start.11
  521.2 2.4 collective-permute-done.11
  525.0 2.5 collective-permute-done.12
  527.5 3.2 collective-permute-start.13
  530.7 2.2 collective-permute-done.13
  533.6 8.2 %shard_map.42 = f32[64,128]{1,0:T(8,128)} custom-call(f32[64,128]{1,0:T(8,128)} %pad_maximum_fusion.3.source_ref), custom_call_target="tpu_custom_call" | custom-call | tf_op jit(solution)/shard_map/pallas_call | solution.py:123
  541.9 11.4 %fusion.116 = f32[64,36864]{1,0:T(8,128)S(1)} fusion(f32[64,36864]{1,0:T(8,128)} %copy-done, f32[64,128]{1,0:T(8,128)} %shard_map.42), kind=kOutput, calls=%fused_computation.198 | convolution fusion | flops 1811939328 | bytes 18907136 | tf_op jit(solution)/shard_map/dot_general | solution.py:78
  554.2 3.0 copy.5
  (56 shorter events, 17.6 us)
Async XLA Ops:
  7.2 418.9 %all-gather.2.cloned.1.call-start = ((), (), s32[]{:S(2)}) async-start(), calls=%async_computation | async-start | bytes 23592960 | tf_op jit(solution)/shard_map/all_gather | solution.py:157
  7.2 11.8 %copy-start.3 = (f32[32,6,48,128]{3,2,1,0:T(8,128)S(1)}, f32[32,6,48,128]{3,2,1,0:T(8,128)}, u32[]{:S(2)}) copy-start(f32[32,6,48,128]{3,2,1,0:T(8,128)} %param.2) | copy-start | bytes 14155780
  7.2 9.3 %collective-permute-start.1 = (f32[32,6,48,128]{3,2,1,0:T(8,128)}, f32[32,6,48,128]{3,2,1,0:T(8,128)S(1)}, u32[]{:S(2)}, u32[]{:S(2)}) collective-permute-start(f32[32,6,48,128]{3,2,1,0:T(8,128)} %param.2), channel_id=1, source_target_pairs={{0,4},{4,8},{8,12},{12,16},{16,20},{20,24},{24,28},{28,32},{32,36}... | collective-permute-start | bytes 14155784 | tf_op jit(solution)/shard_map/ppermute | solution.py:29
  9.1 12.9 %collective-permute-start = (f32[32,6,48,128]{3,2,1,0:T(8,128)}, f32[32,6,48,128]{3,2,1,0:T(8,128)S(1)}, u32[]{:S(2)}, u32[]{:S(2)}) collective-permute-start(f32[32,6,48,128]{3,2,1,0:T(8,128)} %param.2), channel_id=1, source_target_pairs={{4,0},{8,4},{12,8},{16,12},{20,16},{24,20},{28,24},{32,28},{36,32}... | collective-permute-start | bytes 14155784 | tf_op jit(solution)/shard_map/ppermute | solution.py:30
  16.5 2.2 copy-start.4
  22.0 6.4 %copy-start.1 = (f32[32,12,48,128]{3,2,1,0:T(8,128)}, f32[32,12,48,128]{3,2,1,0:T(8,128)S(1)}, u32[]{:S(2)}) copy-start(f32[32,12,48,128]{3,2,1,0:T(8,128)S(1)} %get-tuple-element.5) | copy-start | bytes 28311556
  22.0 2.2 copy-start.5
  24.2 4.2 copy-start.6
  54.8 55.7 %collective-permute-start.2 = (f32[32,6,48,128]{3,2,1,0:T(8,128)}, f32[32,6,48,128]{3,2,1,0:T(8,128)}, u32[]{:S(2)}, u32[]{:S(2)}) collective-permute-start(f32[32,6,48,128]{3,2,1,0:T(8,128)} %get-tuple-element.2), channel_id=1, source_target_pairs={{4,0},{8,4},{12,8},{16,12},{20,16},{24,20},{28,24},{32,28},{36,32}... | collective-permute-start | bytes 14155784 | tf_op jit(solution)/shard_map/ppermute | solution.py:30
  56.1 56.5 %collective-permute-start.3 = (f32[32,6,48,128]{3,2,1,0:T(8,128)}, f32[32,6,48,128]{3,2,1,0:T(8,128)}, u32[]{:S(2)}, u32[]{:S(2)}) collective-permute-start(f32[32,6,48,128]{3,2,1,0:T(8,128)} %get-tuple-element.2), channel_id=1, source_target_pairs={{0,4},{4,8},{8,12},{12,16},{16,20},{20,24},{24,28},{28,32},{32,36}... | collective-permute-start | bytes 14155784 | tf_op jit(solution)/shard_map/ppermute | solution.py:29
  449.7 1.3 collective-permute-start.4
  451.0 3.9 collective-permute-start.5
  454.9 5.4 collective-permute-start.6
  460.3 4.1 collective-permute-start.7
  464.4 5.4 collective-permute-start.8
  478.8 11.3 %copy-start.7 = (f32[64,192]{1,0:T(8,128)S(1)}, f32[64,192]{1,0:T(8,128)}, u32[]{:S(2)}) copy-start(f32[64,192]{1,0:T(8,128)} %shard_map.41) | copy-start | bytes 147460
  490.2 15.3 %copy-start.2 = (f32[64,36864]{1,0:T(8,128)}, f32[64,36864]{1,0:T(8,128)S(1)}, u32[]{:S(2)}) copy-start(f32[64,36864]{1,0:T(8,128)S(1)} %fusion) | copy-start | bytes 28311556
  505.5 7.5 %copy-start = (f32[64,36864]{1,0:T(8,128)}, f32[64,36864]{1,0:T(8,128)S(1)}, u32[]{:S(2)}) copy-start(f32[64,36864]{1,0:T(8,128)S(1)} %convolution_subtract_fusion) | copy-start | bytes 28311556
  512.9 1.3 collective-permute-start.9
  514.2 3.9 collective-permute-start.10
  518.1 5.4 collective-permute-start.11
  523.6 3.9 collective-permute-start.12
  527.5 5.4 collective-permute-start.13
  532.9 20.3 %slice-start = ((s8[9437184]{0:T(1024)(128)(4,1)}), s8[1048576]{0:T(1024)(128)(4,1)S(1)}, s32[]{:S(2)}) async-start(s8[9437184]{0:T(1024)(128)(4,1)} %bitcast.15), calls=%async_computation.1 | async-start | bytes 2097152
  541.9 11.4 %slice-start.1 = ((s8[9437184]{0:T(1024)(128)(4,1)}), s8[4194304]{0:T(1024)(128)(4,1)S(1)}, s32[]{:S(2)}) async-start(s8[9437184]{0:T(1024)(128)(4,1)} %bitcast.15), calls=%async_computation.2 | async-start | bytes 8388608
  541.9 11.4 %slice-start.2 = ((s8[9437184]{0:T(1024)(128)(4,1)}), s8[4194304]{0:T(1024)(128)(4,1)S(1)}, s32[]{:S(2)}) async-start(s8[9437184]{0:T(1024)(128)(4,1)} %bitcast.15), calls=%async_computation.3 | async-start | bytes 8388608
  554.1 3.0 slice-start.3
  554.2 3.0 copy-start.8
Sparse Core Ops, SparseCore 0:
  202.7 223.2 all-gather.1

commit v2 on v1

--- a/solution.py
+++ b/solution.py
@@ -96,6 +96,10 @@
     return value
 
 
+def cell_sum(value):
+    return exchange_sum(exchange_sum(value, "grid"), "orb")
+
+
 def eliminate_kernel(source_ref, result_ref):
     result_ref[...] = source_ref[...]
     rows, width = result_ref.shape
@@ -128,7 +132,7 @@
 
 def factorize(rows_block, inv_cells):
     panel_rows = rows_block.shape[0] // 2
-    leading = exchange_sum(gram_matrix(rows_block[:panel_rows], rows_block), "grid") * inv_cells
+    leading = cell_sum(gram_matrix(rows_block[:panel_rows], rows_block)) * inv_cells
     eye = jnp.eye(panel_rows, dtype=jnp.float32)
     first = eliminate(leading, eye)
     first_r = first[:, :panel_rows]
@@ -136,7 +140,7 @@
     first_lower_inv = first[:, 2 * panel_rows :]
     first_q = mix_rows(first_lower_inv, rows_block[:panel_rows])
     remainder = rows_block[panel_rows:] - apply_rows(coupling, first_q)
-    trailing = exchange_sum(gram_matrix(remainder, remainder), "grid") * inv_cells
+    trailing = cell_sum(gram_matrix(remainder, remainder)) * inv_cells
     second = eliminate(trailing, eye)
     second_r = second[:, :panel_rows]
     second_lower_inv = second[:, panel_rows:]
@@ -154,11 +158,11 @@
     filtered = 2.0 * (hamiltonian(first, potential) - centre * first) / radius - orbital_block
     filtered = filtered.reshape(orb_rows, -1)
     inv_cells = 1.0 / (lax.axis_size("grid") * filtered.shape[1])
-    gathered = lax.all_gather(filtered, "orb", axis=0, tiled=True)
-    triangle, first_q, second_lower_inv, remainder = factorize(gathered, inv_cells)
+    spread = lax.all_to_all(filtered, "orb", 1, 0, tiled=True)
+    triangle, first_q, second_lower_inv, remainder = factorize(spread, inv_cells)
     second_q = mix_rows(second_lower_inv, remainder)
     orbitals = jnp.concatenate([first_q, second_q], axis=0)
-    orbitals = lax.dynamic_slice_in_dim(orbitals, lax.axis_index("orb") * orb_rows, orb_rows, 0)
+    orbitals = lax.all_to_all(orbitals, "orb", 0, 1, tiled=True)
     return (orbitals.reshape(orbital_block.shape), triangle)
 
 

time: 569 us -> 472 us (0.83)
  waiting for transfers between devices: 256 us -> 94.4 us
  starting transfers between devices: 74.3 us -> 155 us
  matrix products: 69 us -> 15.4 us
  blocking collectives: 0 us -> 35.7 us
  local copies, waits for them, and re-layouts: 22.2 us -> 39.7 us
  between operations: 14.5 us -> 0.83 us
    all_gather x1 -> x0, waiting for transfers between devices: 223 us -> none  [local(): gathered = lax.all_gather(filtered, 'orb', axis=0, tiled=True)]
    ppermute x10 -> x14, starting transfers between devices: 18.5 us -> 94.9 us  [exchange_sum(): value = value + lax.ppermute(value, axis, pairs)]
    all_to_all x0 -> x1, waiting for transfers between devices: none -> 48.1 us  [local(): orbitals = lax.all_to_all(orbitals, 'orb', 0, 1, tiled=True)]
    all_to_all x0 -> x1, blocking collectives: none -> 35.7 us  [local(): spread = lax.all_to_all(filtered, 'orb', 1, 0, tiled=True)]
    dot_general x2, matrix products: 31.1 us -> 6.96 us  [gram_matrix(): lax.dot_general(left_rows, right_rows, (((1,), (1,)), ((), ())), precisio...]
    all_to_all x0 -> x3, local copies, waits for them, and re-layouts: none -> 19.3 us  [the longest x2 11.7 us: local(): spread = lax.all_to_all(filtered, 'orb', 1, 0, tiled=True)]
    dot_general x2, matrix products: 22.7 us -> 6.16 us  [mix_rows(): lax.dot_general(weights, source_rows, (((1,), (0,)), ((), ())), precision...]
    dot_general x1, matrix products: 15.3 us -> 2.28 us  [apply_rows(): lax.dot_general(inverse, source_rows, (((0,), (0,)), ((), ())), precision...]
  transfers between devices with their start and end apart: 15 -> 19, of which waited for: 14 -> 18; matrix products, arithmetic and copies ran while one was open for 1% -> 1% of each run, Pallas kernels for 0% -> 0%
where the time goes in v2:
time: 472 us
  starting transfers between devices  155 us (33%)
  other arithmetic  114 us (24%)
  waiting for transfers between devices  94.4 us (20%)
  local copies, waits for them, and re-layouts  39.7 us (8%)
  blocking collectives  35.7 us (8%)
  Pallas kernels  16.4 us (3%)
  matrix products  15.4 us (3%)
    ppermute x14, starting transfers between devices, exchange_sum(): value = value + lax.ppermute(value, axis, pairs)  94.9 us
    sub x1, other arithmetic, local(): 2.0 * (hamiltonian(first, potential) - centre * first) / radius  82.7 us
    ppermute x2, starting transfers between devices, padded_2(): before = lax.ppermute(last, axis, up)  52.7 us
    all_to_all x1, waiting for transfers between devices, local(): orbitals = lax.all_to_all(orbitals, 'orb', 0, 1, tiled=True)  48.1 us
    all_to_all x1, blocking collectives, local(): spread = lax.all_to_all(filtered, 'orb', 1, 0, tiled=True)  35.7 us
    ppermute x14, waiting for transfers between devices, exchange_sum(): value = value + lax.ppermute(value, axis, pairs)  34.5 us
    div x1, other arithmetic, local(): (hamiltonian(orbital_block, potential) - centre * orbital_block) / radius  26.5 us
    pallas_call x2, Pallas kernels, eliminate(): pl.pallas_call(eliminate_kernel, out_shape=jax.ShapeDtypeStruct(source.sh...  16.4 us
  transfers between devices with their start and end apart: 19, of which 18 were waited for; matrix products, arithmetic and copies ran while one was open for 1% of the time, Pallas kernels for 0%

profile of v2, /device:TPU:0, one launch (start us, length us, event | category | flops | bytes accessed | tf_op | source)
XLA Modules:
  0.0 471.6 jit_solution(10496301749435346125)
XLA Ops:
  3.8 6.1 %collective-permute-done.1 = f32[32,6,48,128]{3,2,1,0:T(8,128)S(1)} collective-permute-done((f32[32,6,48,128]{3,2,1,0:T(8,128)}, f32[32,6,48,128]{3,2,1,0:T(8,128)S(1)}, u32[]{:S(2)}, u32[]{:S(2)}) %collective-permute-start.1) | collective-permute-done | bytes 4718624 | tf_op jit(solution)/shard_map/ppermute | solution.py:29
  12.4 3.0 constant_dynamic-update-slice_fusion.1
  17.7 3.0 constant_dynamic-update-slice_fusion
  21.9 26.5 %broadcast_multiply_fusion = (f32[32,6,48,128]{3,2,1,0:T(8,128)}, f32[32,6,48,128]{3,2,1,0:T(8,128)}) fusion(f32[32,6,48,128]{3,2,1,0:T(8,128)S(1)} %copy-done.1, f32[6,48,128]{2,1,0:T(8,128)S(1)} %copy-done.7, f32[32,6,48,128]{3,2,1,0:T(8,128)} %copy-done.5, f32[32,6,48,128]{3,2,1,0:T(8,128)} %copy-done.4, f32[32,12,48,128]{3,2,1,0:T(8,128)} %copy-done, ...), kind=kLoop, calls=%fused_computation.185 | loop fusion | flops 71958528 | bytes 70926336 | tf_op jit(solution)/shard_map/div | solution.py:157
  49.7 50.8 %collective-permute-start.3 = (f32[32,6,48,128]{3,2,1,0:T(8,128)}, f32[32,6,48,128]{3,2,1,0:T(8,128)}, u32[]{:S(2)}, u32[]{:S(2)}) collective-permute-start(f32[32,6,48,128]{3,2,1,0:T(8,128)} %get-tuple-element.2), channel_id=1, source_target_pairs={{0,4},{4,8},{8,12},{12,16},{16,20},{20,24},{24,28},{28,32},{32,36}... | collective-permute-start | bytes 14155784 | tf_op jit(solution)/shard_map/ppermute | solution.py:29
  100.5 3.6 collective-permute-done.2
  106.1 82.7 %multiply_subtract_fusion = f32[32,6,48,128]{3,2,1,0:T(8,128)} fusion(f32[32,6,48,128]{3,2,1,0:T(8,128)} %param.2, f32[32,6,48,128]{3,2,1,0:T(8,128)} %get-tuple-element.3, f32[32,6,48,128]{3,2,1,0:T(8,128)} %get-tuple-element.2, f32[32,6,48,128]{3,2,1,0:T(8,128)} %collective-permute-done.2, f32[32,6,48,128]{3,2,1,0:T(8,128)} %collective-permute-done.3, ...), kind=kLoop, calls=%fused_computation.183 | loop fusion | flops 84934656 | bytes 28459008 | tf_op jit(solution)/shard_map/sub | solution.py:158
  188.8 6.6 %all_to_all.26 = f32[32,4,9216]{2,1,0:T(4,128)} reshape(f32[32,6,48,128]{3,2,1,0:T(8,128)} %multiply_subtract_fusion) | data formatting | bytes 9437184 | tf_op jit(solution)/shard_map/all_to_all | solution.py:161
  195.5 5.1 %copy.4 = f32[32,4,9216]{2,0,1:T(8,128)S(1)} copy(f32[32,4,9216]{2,1,0:T(4,128)} %all_to_all.26) | data formatting | bytes 9437184 | tf_op jit(solution)/shard_map/all_to_all | solution.py:161
  200.6 35.7 %all_to_all.35 = f32[32,4,9216]{2,0,1:T(8,128)S(1)} all-to-all(f32[32,4,9216]{2,0,1:T(8,128)S(1)} %copy.4), channel_id=1, replica_groups=mesh['grid'=32,'orb'=4] {'orb'}, dimensions={1} | all-to-all | bytes 9437184 | tf_op jit(solution)/shard_map/all_to_all | solution.py:161
  238.0 5.0 %fusion.117 = f32[64,128]{1,0:T(8,128)S(1)} fusion(f32[64,9216]{1,0:T(8,128)S(1)} %bitcast.19, f32[128,9216]{1,0:T(8,128)S(1)} %bitcast.18), kind=kOutput, calls=%fused_computation.205 | convolution fusion | flops 905969664 | bytes 7110656 | tf_op jit(solution)/shard_map/dot_general | solution.py:58
  243.0 44.5 %collective-permute-start.4 = (f32[64,128]{1,0:T(8,128)S(1)}, f32[64,128]{1,0:T(8,128)S(1)}, u32[]{:S(2)}, u32[]{:S(2)}) collective-permute-start(f32[64,128]{1,0:T(8,128)S(1)} %fusion.117), channel_id=1, source_target_pairs={{0,4},{4,0},{8,12},{12,8},{16,20},{20,16},{24,28},{28,24},{32,36},... | collective-permute-start | bytes 98312 | tf_op jit(solution)/shard_map/ppermute | solution.py:94
  288.4 27.4 %collective-permute-start.5 = (f32[64,128]{1,0:T(8,128)S(1)}, f32[64,128]{1,0:T(8,128)S(1)}, u32[]{:S(2)}, u32[]{:S(2)}) collective-permute-start(f32[64,128]{1,0:T(8,128)S(1)} %add.344), channel_id=1, source_target_pairs={{0,8},{4,12},{8,0},{12,4},{16,24},{20,28},{24,16},{28,20},{32,40},... | collective-permute-start | bytes 98312 | tf_op jit(solution)/shard_map/ppermute | solution.py:94
  317.7 4.6 collective-permute-start.6
  328.1 3.3 collective-permute-start.8
  334.1 3.3 collective-permute-done.9
  338.5 4.3 collective-permute-done.10
  343.5 8.4 %shard_map.41 = f32[64,192]{1,0:T(8,128)} custom-call(f32[64,192]{1,0:T(8,128)} %pad_maximum_fusion.3.source_ref), custom_call_target="tpu_custom_call" | custom-call | tf_op jit(solution)/shard_map/pallas_call | solution.py:127
  351.9 3.1 fusion.113
  362.0 2.5 collective-permute-done.12
  364.5 3.8 collective-permute-start.13
  371.7 2.4 collective-permute-done.14
  374.1 3.0 collective-permute-start.15
  380.1 3.3 collective-permute-done.16
  384.6 4.3 collective-permute-done.17
  389.6 8.0 %shard_map.42 = f32[64,128]{1,0:T(8,128)} custom-call(f32[64,128]{1,0:T(8,128)} %pad_maximum_fusion.4.source_ref), custom_call_target="tpu_custom_call" | custom-call | tf_op jit(solution)/shard_map/pallas_call | solution.py:127
  397.6 3.1 fusion.110
  400.7 2.5 pad_maximum_fusion.2
  403.2 5.3 %all-to-all-start.1 = ((f32[4,32,9216]{2,1,0:T(8,128)}), f32[4,32,9216]{2,1,0:T(8,128)}, u32[]{:S(2)}, u32[]{:S(2)}) async-start(f32[4,32,9216]{2,1,0:T(8,128)} %bitcast.21), calls=%async_computation.1 | async-start | bytes 9437184 | tf_op jit(solution)/shard_map/all_to_all | solution.py:165
  409.3 48.1 %all-to-all-done.1 = f32[4,32,9216]{2,1,0:T(8,128)} async-done(((f32[4,32,9216]{2,1,0:T(8,128)}), f32[4,32,9216]{2,1,0:T(8,128)}, u32[]{:S(2)}, u32[]{:S(2)}) %all-to-all-start.1) | async-done | bytes 4718624 | tf_op jit(solution)/shard_map/all_to_all | solution.py:165
  457.4 7.6 %copy.5 = f32[32,4,9216]{2,1,0:T(4,128)} copy(f32[32,4,9216]{2,0,1:T(8,128)} %bitcast.5) | data formatting | bytes 9437184 | tf_op jit(solution)/shard_map/all_to_all | solution.py:165
  464.9 6.6 %reshape.19 = f32[32,6,48,128]{3,2,1,0:T(8,128)} reshape(f32[32,4,9216]{2,1,0:T(4,128)} %copy.5) | data formatting | bytes 9437184 | tf_op jit(solution)/shard_map/reshape | solution.py:166
  (66 shorter events, 43.0 us)
Async XLA Ops:
  0.6 11.8 %copy-start.1 = (f32[32,6,48,128]{3,2,1,0:T(8,128)S(1)}, f32[32,6,48,128]{3,2,1,0:T(8,128)}, u32[]{:S(2)}) copy-start(f32[32,6,48,128]{3,2,1,0:T(8,128)} %param.2) | copy-start | bytes 14155780
  0.6 9.3 %collective-permute-start.1 = (f32[32,6,48,128]{3,2,1,0:T(8,128)}, f32[32,6,48,128]{3,2,1,0:T(8,128)S(1)}, u32[]{:S(2)}, u32[]{:S(2)}) collective-permute-start(f32[32,6,48,128]{3,2,1,0:T(8,128)} %param.2), channel_id=1, source_target_pairs={{0,4},{4,8},{8,12},{12,16},{16,20},{20,24},{24,28},{28,32},{32,36}... | collective-permute-start | bytes 14155784 | tf_op jit(solution)/shard_map/ppermute | solution.py:29
  2.5 13.0 %collective-permute-start = (f32[32,6,48,128]{3,2,1,0:T(8,128)}, f32[32,6,48,128]{3,2,1,0:T(8,128)S(1)}, u32[]{:S(2)}, u32[]{:S(2)}) collective-permute-start(f32[32,6,48,128]{3,2,1,0:T(8,128)} %param.2), channel_id=1, source_target_pairs={{4,0},{8,4},{12,8},{16,12},{20,16},{24,20},{28,24},{32,28},{36,32}... | collective-permute-start | bytes 14155784 | tf_op jit(solution)/shard_map/ppermute | solution.py:30
  9.9 2.2 copy-start.4
  15.5 6.4 %copy-start = (f32[32,12,48,128]{3,2,1,0:T(8,128)}, f32[32,12,48,128]{3,2,1,0:T(8,128)S(1)}, u32[]{:S(2)}) copy-start(f32[32,12,48,128]{3,2,1,0:T(8,128)S(1)} %get-tuple-element.7) | copy-start | bytes 28311556
  15.5 2.2 copy-start.5
  17.7 4.2 copy-start.7
  48.4 55.7 %collective-permute-start.2 = (f32[32,6,48,128]{3,2,1,0:T(8,128)}, f32[32,6,48,128]{3,2,1,0:T(8,128)}, u32[]{:S(2)}, u32[]{:S(2)}) collective-permute-start(f32[32,6,48,128]{3,2,1,0:T(8,128)} %get-tuple-element.2), channel_id=1, source_target_pairs={{4,0},{8,4},{12,8},{16,12},{20,16},{24,20},{28,24},{32,28},{36,32}... | collective-permute-start | bytes 14155784 | tf_op jit(solution)/shard_map/ppermute | solution.py:30
  49.7 56.5 %collective-permute-start.3 = (f32[32,6,48,128]{3,2,1,0:T(8,128)}, f32[32,6,48,128]{3,2,1,0:T(8,128)}, u32[]{:S(2)}, u32[]{:S(2)}) collective-permute-start(f32[32,6,48,128]{3,2,1,0:T(8,128)} %get-tuple-element.2), channel_id=1, source_target_pairs={{0,4},{4,8},{8,12},{12,16},{16,20},{20,24},{24,28},{28,32},{32,36}... | collective-permute-start | bytes 14155784 | tf_op jit(solution)/shard_map/ppermute | solution.py:29
  243.0 45.4 %collective-permute-start.4 = (f32[64,128]{1,0:T(8,128)S(1)}, f32[64,128]{1,0:T(8,128)S(1)}, u32[]{:S(2)}, u32[]{:S(2)}) collective-permute-start(f32[64,128]{1,0:T(8,128)S(1)} %fusion.117), channel_id=1, source_target_pairs={{0,4},{4,0},{8,12},{12,8},{16,20},{20,16},{24,28},{28,24},{32,36},... | collective-permute-start | bytes 98312 | tf_op jit(solution)/shard_map/ppermute | solution.py:94
  288.4 29.3 %collective-permute-start.5 = (f32[64,128]{1,0:T(8,128)S(1)}, f32[64,128]{1,0:T(8,128)S(1)}, u32[]{:S(2)}, u32[]{:S(2)}) collective-permute-start(f32[64,128]{1,0:T(8,128)S(1)} %add.344), channel_id=1, source_target_pairs={{0,8},{4,12},{8,0},{12,4},{16,24},{20,28},{24,16},{28,20},{32,40},... | collective-permute-start | bytes 98312 | tf_op jit(solution)/shard_map/ppermute | solution.py:94
  317.7 6.5 %collective-permute-start.6 = (f32[64,128]{1,0:T(8,128)S(1)}, f32[64,128]{1,0:T(8,128)S(1)}, u32[]{:S(2)}, u32[]{:S(2)}) collective-permute-start(f32[64,128]{1,0:T(8,128)S(1)} %add.345), channel_id=1, source_target_pairs={{0,16},{4,20},{8,24},{12,28},{16,0},{20,4},{24,8},{28,12},{32,48},... | collective-permute-start | bytes 98312 | tf_op jit(solution)/shard_map/ppermute | solution.py:94
  324.2 3.9 collective-permute-start.7
  328.1 5.4 %collective-permute-start.8 = (f32[64,128]{1,0:T(8,128)S(1)}, f32[64,128]{1,0:T(8,128)S(1)}, u32[]{:S(2)}, u32[]{:S(2)}) collective-permute-start(f32[64,128]{1,0:T(8,128)S(1)} %add.347), channel_id=1, source_target_pairs={{0,64},{4,68},{8,72},{12,76},{16,80},{20,84},{24,88},{28,92},{32,9... | collective-permute-start | bytes 98312 | tf_op jit(solution)/shard_map/ppermute | solution.py:94
  333.5 3.9 collective-permute-start.9
  337.4 5.4 %collective-permute-start.10 = (f32[64,128]{1,0:T(8,128)S(1)}, f32[64,128]{1,0:T(8,128)S(1)}, u32[]{:S(2)}, u32[]{:S(2)}) collective-permute-start(f32[64,128]{1,0:T(8,128)S(1)} %add.349), channel_id=1, source_target_pairs={{0,2},{1,3},{2,0},{3,1},{4,6},{5,7},{6,4},{7,5},{8,10},{9,11},{10,... | collective-permute-start | bytes 98312 | tf_op jit(solution)/shard_map/ppermute | solution.py:94
  351.9 3.1 copy-start.6
  351.9 3.1 copy-start.8
  355.0 4.3 copy-start.2
  359.3 1.3 collective-permute-start.11
  360.6 3.9 collective-permute-start.12
  364.5 5.7 %collective-permute-start.13 = (f32[64,64]{1,0:T(8,128)S(1)}, f32[64,64]{1,0:T(8,128)S(1)}, u32[]{:S(2)}, u32[]{:S(2)}) collective-permute-start(f32[64,64]{1,0:T(8,128)S(1)} %add.352), channel_id=1, source_target_pairs={{0,16},{4,20},{8,24},{12,28},{16,0},{20,4},{24,8},{28,12},{32,48},... | collective-permute-start | bytes 49160 | tf_op jit(solution)/shard_map/ppermute | solution.py:94
  370.2 3.9 collective-permute-start.14
  374.1 5.4 %collective-permute-start.15 = (f32[64,64]{1,0:T(8,128)S(1)}, f32[64,64]{1,0:T(8,128)S(1)}, u32[]{:S(2)}, u32[]{:S(2)}) collective-permute-start(f32[64,64]{1,0:T(8,128)S(1)} %add.354), channel_id=1, source_target_pairs={{0,64},{4,68},{8,72},{12,76},{16,80},{20,84},{24,88},{28,92},{32,9... | collective-permute-start | bytes 49160 | tf_op jit(solution)/shard_map/ppermute | solution.py:94
  379.6 3.9 collective-permute-start.16
  383.5 5.4 %collective-permute-start.17 = (f32[64,64]{1,0:T(8,128)S(1)}, f32[64,64]{1,0:T(8,128)S(1)}, u32[]{:S(2)}, u32[]{:S(2)}) collective-permute-start(f32[64,64]{1,0:T(8,128)S(1)} %add.356), channel_id=1, source_target_pairs={{0,2},{1,3},{2,0},{3,1},{4,6},{5,7},{6,4},{7,5},{8,10},{9,11},{10,... | collective-permute-start | bytes 49160 | tf_op jit(solution)/shard_map/ppermute | solution.py:94
  397.6 3.1 copy-start.3
  403.2 5.3 %slice-start = ((f32[64,192]{1,0:T(8,128)}), f32[64,128]{1,0:T(8,128)S(1)}, s32[]{:S(2)}) async-start(f32[64,192]{1,0:T(8,128)} %shard_map.41), calls=%async_computation.2 | async-start | bytes 65536 | tf_op jit(solution)/shard_map/concatenate | solution.py:147
  403.2 5.3 %copy-start.9 = (f32[64,128]{1,0:T(8,128)S(1)}, f32[64,128]{1,0:T(8,128)}, u32[]{:S(2)}) copy-start(f32[64,128]{1,0:T(8,128)} %shard_map.42) | copy-start | bytes 98308
  403.2 54.1 %all-to-all-start.1 = ((f32[4,32,9216]{2,1,0:T(8,128)}), f32[4,32,9216]{2,1,0:T(8,128)}, u32[]{:S(2)}, u32[]{:S(2)}) async-start(f32[4,32,9216]{2,1,0:T(8,128)} %bitcast.21), calls=%async_computation.1 | async-start | bytes 9437184 | tf_op jit(solution)/shard_map/all_to_all | solution.py:165

commit v3 on v2

--- a/solution.py
+++ b/solution.py
@@ -19,30 +19,23 @@
 highest = lax.Precision.HIGHEST
 
 
-def padded_2(value, sides, width):
-    for axis, dim in sides:
-        size, length = (lax.axis_size(axis), value.shape[dim])
-        up = [(i, (i + 1) % size) for i in range(size - 1)]
-        down = [(j, i) for i, j in up]
-        last = lax.slice_in_dim(value, length - width, length, axis=dim)
-        first = lax.slice_in_dim(value, 0, width, axis=dim)
-        before = lax.ppermute(last, axis, up)
-        after = lax.ppermute(first, axis, down)
-        value = jnp.concatenate([before, value, after], axis=dim)
-    return value
+def halo_planes(value, axis, width):
+    size, length = (lax.axis_size(axis), value.shape[1])
+    up = [(i, (i + 1) % size) for i in range(size - 1)]
+    down = [(j, i) for i, j in up]
+    last = lax.slice_in_dim(value, length - width, length, axis=1)
+    first = lax.slice_in_dim(value, 0, width, axis=1)
+    before = lax.ppermute(last, axis, up)
+    after = lax.ppermute(first, axis, down)
+    return before, after
 
 
-def hamiltonian(orbital_field, potential):
-    slab_cells = orbital_field.shape[1]
+def local_terms(orbital_field, potential):
     across = orbital_field.shape[2]
     depth_cells = orbital_field.shape[3]
-    widened = padded_2(orbital_field, (("grid", 1),), 6)
     padded = jnp.pad(orbital_field, ((0, 0), (0, 0), (6, 6), (6, 6)))
     total = 3.0 * coefs[0] * orbital_field
     for k in range(1, 7):
-        total = total + coefs[k] * (
-            widened[:, 6 + k : 6 + k + slab_cells] + widened[:, 6 - k : 6 - k + slab_cells]
-        )
         total = total + coefs[k] * (
             padded[:, :, 6 + k : 6 + k + across, 6 : 6 + depth_cells]
             + padded[:, :, 6 - k : 6 - k + across, 6 : 6 + depth_cells]
@@ -54,11 +47,35 @@
     return -2.0 * total + potential[None] * orbital_field
 
 
+def slab_terms(orbital_field, before, after):
+    width = before.shape[1]
+    planes = (
+        [before[:, q] for q in range(width)]
+        + [orbital_field[:, q] for q in range(orbital_field.shape[1])]
+        + [after[:, q] for q in range(width)]
+    )
+    rows = []
+    for p in range(orbital_field.shape[1]):
+        centre_plane = width + p
+        acc = coefs[1] * (planes[centre_plane + 1] + planes[centre_plane - 1])
+        for k in range(2, 7):
+            acc = acc + coefs[k] * (planes[centre_plane + k] + planes[centre_plane - k])
+        rows.append(acc)
+    return jnp.stack(rows, axis=1)
+
+
+def hamiltonian(orbital_field, potential):
+    before, after = halo_planes(orbital_field, "grid", 6)
+    local = local_terms(orbital_field, potential)
+    local, before, after = lax.optimization_barrier((local, before, after))
+    return local - 2.0 * slab_terms(orbital_field, before, after)
+
+
 def gram_matrix(left_rows, right_rows):
     return lax.dot_general(
         left_rows,
         right_rows,
-        (((1,), (1,)), ((), ())),
+        (((1, 2), (1, 2)), ((), ())),
         precision=highest,
         preferred_element_type=jnp.float32,
     )
@@ -156,12 +173,16 @@
     orb_rows = orbital_block.shape[0]
     first = (hamiltonian(orbital_block, potential) - centre * orbital_block) / radius
     filtered = 2.0 * (hamiltonian(first, potential) - centre * first) / radius - orbital_block
-    filtered = filtered.reshape(orb_rows, -1)
-    inv_cells = 1.0 / (lax.axis_size("grid") * filtered.shape[1])
-    spread = lax.all_to_all(filtered, "orb", 1, 0, tiled=True)
+    parts = lax.axis_size("orb")
+    lanes = orbital_block.shape[3]
+    rows_per_part = orbital_block.shape[1] * orbital_block.shape[2] // parts
+    filtered = filtered.reshape(orb_rows, parts, rows_per_part, lanes)
+    inv_cells = 1.0 / (lax.axis_size("grid") * parts * rows_per_part * lanes)
+    spread = lax.all_to_all(filtered, "orb", 1, 0, tiled=True).reshape(-1, rows_per_part, lanes)
     triangle, first_q, second_lower_inv, remainder = factorize(spread, inv_cells)
     second_q = mix_rows(second_lower_inv, remainder)
     orbitals = jnp.concatenate([first_q, second_q], axis=0)
+    orbitals = orbitals.reshape(orbitals.shape[0], 1, rows_per_part, lanes)
     orbitals = lax.all_to_all(orbitals, "orb", 0, 1, tiled=True)
     return (orbitals.reshape(orbital_block.shape), triangle)
 

time: 472 us -> 406 us (0.86); the launches traced: 472 us -> 399 us
  starting transfers between devices: 155 us -> 101 us
  local copies, waits for them, and re-layouts: 39.7 us -> 16 us
  other arithmetic: 114 us -> 132 us
  waiting for transfers between devices: 94.4 us -> 81.4 us
    sub x1, other arithmetic: 82.7 us -> 7.1 us  [local(): 2.0 * (hamiltonian(first, potential) - centre * first) / radius]
    add x0 -> x2, other arithmetic: none -> 69.7 us  [local_terms(): return -2.0 * total + potential[None] * orbital_field]
    ppermute x4, starting transfers between devices: 55.2 us -> 12.7 us  [the longest x2 9.97 us: halo_planes(): before = lax.ppermute(last, axis, up)]
    unnamed x0 -> x10, other arithmetic: none -> 36.7 us
    div x1, other arithmetic: 26.5 us -> 7.44 us  [local(): (hamiltonian(orbital_block, potential) - centre * orbital_block) / radius]
    ppermute x14, starting transfers between devices: 94.9 us -> 82.7 us  [exchange_sum(): value = value + lax.ppermute(value, axis, pairs)]
    ppermute x4, waiting for transfers between devices: 11.8 us -> 0.01 us  [the longest x2 0.01 us: halo_planes(): before = lax.ppermute(last, axis, up)]
    all_to_all x2 -> x1, local copies, waits for them, and re-layouts: 11.7 us -> 0.74 us  [local(): lax.all_to_all(filtered, 'orb', 1, 0, tiled=True)]
  transfers between devices with their start and end apart: 19 -> 19, of which waited for: 18 -> 15; matrix products, arithmetic and copies ran while one was open for 1% -> 18% of each run, Pallas kernels for 0% -> 0%
where the time goes in v3:
time: 406 us; the launch traced here: 399 us
  other arithmetic  132 us (33%)
  starting transfers between devices  101 us (25%)
  waiting for transfers between devices  81.4 us (20%)
  blocking collectives  35.9 us (9%)
  Pallas kernels  16.4 us (4%)
  local copies, waits for them, and re-layouts  16 us (4%)
  matrix products  15.4 us (4%)
    ppermute x14, starting transfers between devices, exchange_sum(): value = value + lax.ppermute(value, axis, pairs)  82.7 us
    add x2, other arithmetic, local_terms(): return -2.0 * total + potential[None] * orbital_field  69.7 us
    all_to_all x1, waiting for transfers between devices, local(): orbitals = lax.all_to_all(orbitals, 'orb', 0, 1, tiled=True)  47.5 us
    unnamed x10, other arithmetic  36.7 us
    all_to_all x1, blocking collectives, local(): lax.all_to_all(filtered, 'orb', 1, 0, tiled=True)  35.9 us
    ppermute x14, waiting for transfers between devices, exchange_sum(): value = value + lax.ppermute(value, axis, pairs)  33.9 us
    pallas_call x2, Pallas kernels, eliminate(): pl.pallas_call(eliminate_kernel, out_shape=jax.ShapeDtypeStruct(source.sh...  16.4 us
    ppermute x2, starting transfers between devices, halo_planes(): before = lax.ppermute(last, axis, up)  9.97 us
  transfers between devices with their start and end apart: 19, of which 15 were waited for; matrix products, arithmetic and copies ran while one was open for 18% of the time, Pallas kernels for 0%

profile of v3, /device:TPU:0, one launch (start us, length us, event | category | flops | bytes accessed | tf_op | source)
XLA Modules:
  0.0 398.6 jit_solution(3233143915988646989)
XLA Ops:
  3.8 52.5 %multiply_add_fusion.1 = f32[32,6,48,128]{3,2,1,0:T(8,128)} fusion(f32[32,6,48,128]{3,2,1,0:T(8,128)} %param.2, f32[6,48,128]{2,1,0:T(8,128)} %param.3), kind=kLoop, calls=%fused_computation.124 | loop fusion | flops 47185920 | bytes 9584640 | tf_op jit(solution)/shard_map/add | solution.py:47
  61.9 3.2 add_dynamic-update-slice_fusion.9
  65.1 3.4 add_dynamic-update-slice_fusion.8
  68.5 3.7 add_dynamic-update-slice_fusion.7
  72.2 3.9 add_dynamic-update-slice_fusion.6
  76.0 7.4 %broadcast_multiply_fusion = (f32[32,6,48,128]{3,2,1,0:T(8,128)S(1)}, f32[32,6,48,128]{3,2,1,0:T(8,128)}) fusion(f32[32,6,48,128]{3,2,1,0:T(8,128)S(1)} %copy-done, f32[32,6,48,128]{3,2,1,0:T(8,128)} %multiply_add_fusion.1, f32[32,6,48,128]{3,2,1,0:T(8,128)} %add_dynamic-update-slice_fusion.6), kind=kLoop, calls=%fused_computation.125 | loop fusion | flops 5898240 | bytes 23592960 | tf_op jit(solution)/shard_map/div | solution.py:174
  83.5 8.1 %collective-permute-start.2 = (f32[32,6,48,128]{3,2,1,0:T(8,128)S(1)}, f32[32,6,48,128]{3,2,1,0:T(8,128)}, u32[]{:S(2)}, u32[]{:S(2)}) collective-permute-start(f32[32,6,48,128]{3,2,1,0:T(8,128)S(1)} %get-tuple-element.14), channel_id=1, source_target_pairs={{0,4},{4,8},{8,12},{12,16},{16,20},{20,24},{24,28},{28,32},{32,36}... | collective-permute-start | bytes 14155784 | tf_op jit(solution)/shard_map/ppermute | solution.py:28
  93.1 17.2 %multiply_add_fusion = f32[32,6,48,128]{3,2,1,0:T(8,128)} fusion(f32[32,6,48,128]{3,2,1,0:T(8,128)} %get-tuple-element.15, f32[32,6,48,128]{3,2,1,0:T(8,128)S(1)} %get-tuple-element.14, f32[6,48,128]{2,1,0:T(8,128)S(1)} %broadcast_multiply_fusion.1), kind=kLoop, calls=%fused_computation.122 | loop fusion | flops 47185920 | bytes 14303232 | tf_op jit(solution)/shard_map/add | solution.py:47
  110.3 4.1 %add_dynamic-update-slice_fusion.5 = f32[32,6,48,128]{3,2,1,0:T(8,128)} fusion(f32[32,6,48,128]{3,2,1,0:T(8,128)} %collective-permute-done.2, f32[32,6,48,128]{3,2,1,0:T(8,128)S(1)} %get-tuple-element.14, f32[32,6,48,128]{3,2,1,0:T(8,128)} %collective-permute-done.3), kind=kLoop, calls=%fused_computation.134 | loop fusion | flops 3342335 | bytes 10223616
  114.4 4.3 %add_dynamic-update-slice_fusion.4 = f32[32,6,48,128]{3,2,1,0:T(8,128)} fusion(f32[32,6,48,128]{3,2,1,0:T(8,128)} %add_dynamic-update-slice_fusion.5, f32[32,6,48,128]{3,2,1,0:T(8,128)} %collective-permute-done.2, f32[32,6,48,128]{3,2,1,0:T(8,128)S(1)} %get-tuple-element.14, f32[32,6,48,128]{3,2,1,0:T(8,128)} %collective-permute-done.3), kind=kLoop, calls=%fused_computation.133 | loop fusion | flops 3342336 | bytes 10223616
  118.7 4.1 %add_dynamic-update-slice_fusion.3 = f32[32,6,48,128]{3,2,1,0:T(8,128)} fusion(f32[32,6,48,128]{3,2,1,0:T(8,128)} %add_dynamic-update-slice_fusion.4, f32[32,6,48,128]{3,2,1,0:T(8,128)} %collective-permute-done.2, f32[32,6,48,128]{3,2,1,0:T(8,128)} %collective-permute-done.3, f32[32,6,48,128]{3,2,1,0:T(8,128)S(1)} %get-tuple-element.14), kind=kLoop, calls=%fused_computation.132 | loop fusion | flops 3342336 | bytes 10223616
  122.8 4.2 %add_dynamic-update-slice_fusion.2 = f32[32,6,48,128]{3,2,1,0:T(8,128)} fusion(f32[32,6,48,128]{3,2,1,0:T(8,128)} %add_dynamic-update-slice_fusion.3, f32[32,6,48,128]{3,2,1,0:T(8,128)} %collective-permute-done.3, f32[32,6,48,128]{3,2,1,0:T(8,128)} %collective-permute-done.2, f32[32,6,48,128]{3,2,1,0:T(8,128)S(1)} %get-tuple-element.14), kind=kLoop, calls=%fused_computation.131 | loop fusion | flops 3342336 | bytes 10223616
  127.0 4.1 %add_dynamic-update-slice_fusion.1 = f32[32,6,48,128]{3,2,1,0:T(8,128)} fusion(f32[32,6,48,128]{3,2,1,0:T(8,128)} %add_dynamic-update-slice_fusion.2, f32[32,6,48,128]{3,2,1,0:T(8,128)} %collective-permute-done.3, f32[32,6,48,128]{3,2,1,0:T(8,128)S(1)} %get-tuple-element.14, f32[32,6,48,128]{3,2,1,0:T(8,128)} %collective-permute-done.2), kind=kLoop, calls=%fused_computation.130 | loop fusion | flops 3342336 | bytes 10223616
  131.1 4.1 %add_dynamic-update-slice_fusion = f32[32,6,48,128]{3,2,1,0:T(8,128)} fusion(f32[32,6,48,128]{3,2,1,0:T(8,128)} %add_dynamic-update-slice_fusion.1, f32[32,6,48,128]{3,2,1,0:T(8,128)} %collective-permute-done.3, f32[32,6,48,128]{3,2,1,0:T(8,128)S(1)} %get-tuple-element.14, f32[32,6,48,128]{3,2,1,0:T(8,128)} %collective-permute-done.2), kind=kLoop, calls=%fused_computation.129 | loop fusion | flops 3342336 | bytes 10223616 | tf_op jit(solution)/shard_map/stack | solution.py:64
  135.3 7.1 %multiply_subtract_fusion = f32[32,6,48,128]{3,2,1,0:T(8,128)S(1)} fusion(f32[32,6,48,128]{3,2,1,0:T(8,128)S(1)} %copy-done, f32[32,6,48,128]{3,2,1,0:T(8,128)} %get-tuple-element.15, f32[32,6,48,128]{3,2,1,0:T(8,128)} %multiply_add_fusion, f32[32,6,48,128]{3,2,1,0:T(8,128)} %add_dynamic-update-slice_fusion), kind=kLoop, calls=%fused_computation.121 | loop fusion | flops 7077888 | bytes 23592960 | tf_op jit(solution)/shard_map/sub | solution.py:175
  145.1 35.9 %all_to_all.30 = f32[32,4,72,128]{3,0,2,1:T(8,128)S(1)} all-to-all(f32[32,4,72,128]{3,0,2,1:T(8,128)S(1)} %bitcast.39), channel_id=1, replica_groups=mesh['grid'=32,'orb'=4] {'orb'}, dimensions={1} | all-to-all | bytes 9437184 | tf_op jit(solution)/shard_map/all_to_all | solution.py:181
  182.5 5.0 %convolution_bitcast_fusion.1 = f32[64,128]{1,0:T(8,128)S(1)} fusion(f32[64,72,128]{2,0,1:T(8,128)S(1)} %bitcast.36, f32[128,72,128]{2,0,1:T(8,128)S(1)} %bitcast.38), kind=kOutput, calls=%fused_computation.128 | convolution fusion | flops 905969664 | bytes 7110656 | tf_op jit(solution)/shard_map/dot_general | solution.py:75
  187.5 33.8 %collective-permute-start.4 = (f32[64,128]{1,0:T(8,128)S(1)}, f32[64,128]{1,0:T(8,128)S(1)}, u32[]{:S(2)}, u32[]{:S(2)}) collective-permute-start(f32[64,128]{1,0:T(8,128)S(1)} %convolution_bitcast_fusion.1), channel_id=1, source_target_pairs={{0,4},{4,0},{8,12},{12,8},{16,20},{20,16},{24,28},{28,24},{32,36},... | collective-permute-start | bytes 98312 | tf_op jit(solution)/shard_map/ppermute | solution.py:111
  222.1 26.1 %collective-permute-start.5 = (f32[64,128]{1,0:T(8,128)S(1)}, f32[64,128]{1,0:T(8,128)S(1)}, u32[]{:S(2)}, u32[]{:S(2)}) collective-permute-start(f32[64,128]{1,0:T(8,128)S(1)} %add.908), channel_id=1, source_target_pairs={{0,8},{4,12},{8,0},{12,4},{16,24},{20,28},{24,16},{28,20},{32,40},... | collective-permute-start | bytes 98312 | tf_op jit(solution)/shard_map/ppermute | solution.py:111
  250.2 4.1 %collective-permute-start.6 = (f32[64,128]{1,0:T(8,128)S(1)}, f32[64,128]{1,0:T(8,128)S(1)}, u32[]{:S(2)}, u32[]{:S(2)}) collective-permute-start(f32[64,128]{1,0:T(8,128)S(1)} %add.909), channel_id=1, source_target_pairs={{0,16},{4,20},{8,24},{12,28},{16,0},{20,4},{24,8},{28,12},{32,48},... | collective-permute-start | bytes 98312 | tf_op jit(solution)/shard_map/ppermute | solution.py:111
  261.0 3.7 collective-permute-start.8
  267.1 3.3 collective-permute-done.9
  276.8 8.4 %shard_map.41 = f32[64,192]{1,0:T(8,128)} custom-call(f32[64,192]{1,0:T(8,128)} %pad_maximum_fusion.source_ref), custom_call_target="tpu_custom_call" | custom-call | tf_op jit(solution)/shard_map/pallas_call | solution.py:144
  294.3 3.5 collective-permute-done.12
  307.1 3.7 collective-permute-start.15
  313.3 3.3 collective-permute-done.16
  317.8 4.6 %collective-permute-done.17 = f32[64,64]{1,0:T(8,128)S(1)} collective-permute-done((f32[64,64]{1,0:T(8,128)S(1)}, f32[64,64]{1,0:T(8,128)S(1)}, u32[]{:S(2)}, u32[]{:S(2)}) %collective-permute-start.17) | collective-permute-done | bytes 16416 | tf_op jit(solution)/shard_map/ppermute | solution.py:111
  323.0 8.0 %shard_map.42 = f32[64,128]{1,0:T(8,128)} custom-call(f32[64,128]{1,0:T(8,128)} %pad_maximum_fusion.1.source_ref), custom_call_target="tpu_custom_call" | custom-call | tf_op jit(solution)/shard_map/pallas_call | solution.py:144
  334.7 4.9 %copy.12 = f32[128,1,72,128]{3,2,1,0:T(8,128)} copy(f32[128,1,72,128]{3,0,2,1:T(8,128)S(1)} %maximum_bitcast_fusion) | data formatting | bytes 9437184 | tf_op jit(solution)/shard_map/reshape | solution.py:185
  339.7 5.1 %all-to-all-start.1 = ((f32[128,1,72,128]{3,2,1,0:T(8,128)}), f32[128,1,72,128]{3,2,1,0:T(8,128)}, u32[]{:S(2)}, u32[]{:S(2)}) async-start(f32[128,1,72,128]{3,2,1,0:T(8,128)} %copy.12), calls=%async_computation.1 | async-start | bytes 9437184 | tf_op jit(solution)/shard_map/all_to_all | solution.py:186
  345.5 47.5 %all-to-all-done.1 = f32[128,1,72,128]{3,2,1,0:T(8,128)} async-done(((f32[128,1,72,128]{3,2,1,0:T(8,128)}), f32[128,1,72,128]{3,2,1,0:T(8,128)}, u32[]{:S(2)}, u32[]{:S(2)}) %all-to-all-start.1) | async-done | bytes 4718624 | tf_op jit(solution)/shard_map/all_to_all | solution.py:186
  393.0 5.1 %copy.13 = f32[32,4,1,72,128]{4,3,1,0,2:T(8,128)} copy(f32[32,4,1,72,128]{4,3,0,1,2:T(8,128)} %bitcast.14) | data formatting | bytes 9437184 | tf_op jit(solution)/shard_map/all_to_all | solution.py:186
  (73 shorter events, 59.8 us)
Async XLA Ops:
  0.6 55.7 %copy-start = (f32[32,6,48,128]{3,2,1,0:T(8,128)S(1)}, f32[32,6,48,128]{3,2,1,0:T(8,128)}, u32[]{:S(2)}) copy-start(f32[32,6,48,128]{3,2,1,0:T(8,128)} %param.2) | copy-start | bytes 14155780
  0.6 55.7 %collective-permute-start = (f32[32,6,48,128]{3,2,1,0:T(8,128)}, f32[32,6,48,128]{3,2,1,0:T(8,128)S(1)}, u32[]{:S(2)}, u32[]{:S(2)}) collective-permute-start(f32[32,6,48,128]{3,2,1,0:T(8,128)} %param.2), channel_id=1, source_target_pairs={{0,4},{4,8},{8,12},{12,16},{16,20},{20,24},{24,28},{28,32},{32,36}... | collective-permute-start | bytes 14155784 | tf_op jit(solution)/shard_map/ppermute | solution.py:28
  2.5 53.8 %collective-permute-start.1 = (f32[32,6,48,128]{3,2,1,0:T(8,128)}, f32[32,6,48,128]{3,2,1,0:T(8,128)}, u32[]{:S(2)}, u32[]{:S(2)}) collective-permute-start(f32[32,6,48,128]{3,2,1,0:T(8,128)} %param.2), channel_id=1, source_target_pairs={{4,0},{8,4},{12,8},{16,12},{20,16},{24,20},{28,24},{32,28},{36,32}... | collective-permute-start | bytes 14155784 | tf_op jit(solution)/shard_map/ppermute | solution.py:29
  76.0 17.0 %copy-start.4 = (f32[6,48,128]{2,1,0:T(8,128)S(1)}, f32[6,48,128]{2,1,0:T(8,128)}, u32[]{:S(2)}) copy-start(f32[6,48,128]{2,1,0:T(8,128)} %param.3) | copy-start | bytes 442372
  83.5 26.8 %collective-permute-start.2 = (f32[32,6,48,128]{3,2,1,0:T(8,128)S(1)}, f32[32,6,48,128]{3,2,1,0:T(8,128)}, u32[]{:S(2)}, u32[]{:S(2)}) collective-permute-start(f32[32,6,48,128]{3,2,1,0:T(8,128)S(1)} %get-tuple-element.14), channel_id=1, source_target_pairs={{0,4},{4,8},{8,12},{12,16},{16,20},{20,24},{24,28},{28,32},{32,36}... | collective-permute-start | bytes 14155784 | tf_op jit(solution)/shard_map/ppermute | solution.py:28
  91.6 18.7 %collective-permute-start.3 = (f32[32,6,48,128]{3,2,1,0:T(8,128)S(1)}, f32[32,6,48,128]{3,2,1,0:T(8,128)}, u32[]{:S(2)}, u32[]{:S(2)}) collective-permute-start(f32[32,6,48,128]{3,2,1,0:T(8,128)S(1)} %get-tuple-element.14), channel_id=1, source_target_pairs={{4,0},{8,4},{12,8},{16,12},{20,16},{24,20},{28,24},{32,28},{36,32}... | collective-permute-start | bytes 14155784 | tf_op jit(solution)/shard_map/ppermute | solution.py:29
  187.5 34.6 %collective-permute-start.4 = (f32[64,128]{1,0:T(8,128)S(1)}, f32[64,128]{1,0:T(8,128)S(1)}, u32[]{:S(2)}, u32[]{:S(2)}) collective-permute-start(f32[64,128]{1,0:T(8,128)S(1)} %convolution_bitcast_fusion.1), channel_id=1, source_target_pairs={{0,4},{4,0},{8,12},{12,8},{16,20},{20,16},{24,28},{28,24},{32,36},... | collective-permute-start | bytes 98312 | tf_op jit(solution)/shard_map/ppermute | solution.py:111
  222.1 28.0 %collective-permute-start.5 = (f32[64,128]{1,0:T(8,128)S(1)}, f32[64,128]{1,0:T(8,128)S(1)}, u32[]{:S(2)}, u32[]{:S(2)}) collective-permute-start(f32[64,128]{1,0:T(8,128)S(1)} %add.908), channel_id=1, source_target_pairs={{0,8},{4,12},{8,0},{12,4},{16,24},{20,28},{24,16},{28,20},{32,40},... | collective-permute-start | bytes 98312 | tf_op jit(solution)/shard_map/ppermute | solution.py:111
  250.2 6.0 %collective-permute-start.6 = (f32[64,128]{1,0:T(8,128)S(1)}, f32[64,128]{1,0:T(8,128)S(1)}, u32[]{:S(2)}, u32[]{:S(2)}) collective-permute-start(f32[64,128]{1,0:T(8,128)S(1)} %add.909), channel_id=1, source_target_pairs={{0,16},{4,20},{8,24},{12,28},{16,0},{20,4},{24,8},{28,12},{32,48},... | collective-permute-start | bytes 98312 | tf_op jit(solution)/shard_map/ppermute | solution.py:111
  256.2 4.8 %collective-permute-start.7 = (f32[64,128]{1,0:T(8,128)S(1)}, f32[64,128]{1,0:T(8,128)S(1)}, u32[]{:S(2)}, u32[]{:S(2)}) collective-permute-start(f32[64,128]{1,0:T(8,128)S(1)} %add.910), channel_id=1, source_target_pairs={{0,32},{4,36},{8,40},{12,44},{16,48},{20,52},{24,56},{28,60},{32,0... | collective-permute-start | bytes 98312 | tf_op jit(solution)/shard_map/ppermute | solution.py:111
  261.0 5.5 %collective-permute-start.8 = (f32[64,128]{1,0:T(8,128)S(1)}, f32[64,128]{1,0:T(8,128)S(1)}, u32[]{:S(2)}, u32[]{:S(2)}) collective-permute-start(f32[64,128]{1,0:T(8,128)S(1)} %add.911), channel_id=1, source_target_pairs={{0,64},{4,68},{8,72},{12,76},{16,80},{20,84},{24,88},{28,92},{32,9... | collective-permute-start | bytes 98312 | tf_op jit(solution)/shard_map/ppermute | solution.py:111
  266.5 3.9 collective-permute-start.9
  270.5 5.6 %collective-permute-start.10 = (f32[64,128]{1,0:T(8,128)S(1)}, f32[64,128]{1,0:T(8,128)S(1)}, u32[]{:S(2)}, u32[]{:S(2)}) collective-permute-start(f32[64,128]{1,0:T(8,128)S(1)} %add.913), channel_id=1, source_target_pairs={{0,2},{1,3},{2,0},{3,1},{4,6},{5,7},{6,4},{7,5},{8,10},{9,11},{10,... | collective-permute-start | bytes 98312 | tf_op jit(solution)/shard_map/ppermute | solution.py:111
  285.1 3.1 copy-start.3
  285.1 3.1 copy-start.5
  288.2 4.3 %copy-start.1 = (f32[64,72,128]{2,0,1:T(8,128)}, f32[64,72,128]{2,0,1:T(8,128)S(1)}, u32[]{:S(2)}) copy-start(f32[64,72,128]{2,0,1:T(8,128)S(1)} %fusion.73) | copy-start | bytes 7077892
  292.5 1.3 collective-permute-start.11
  293.8 3.9 collective-permute-start.12
  297.8 5.4 %collective-permute-start.13 = (f32[64,64]{1,0:T(8,128)S(1)}, f32[64,64]{1,0:T(8,128)S(1)}, u32[]{:S(2)}, u32[]{:S(2)}) collective-permute-start(f32[64,64]{1,0:T(8,128)S(1)} %add.916), channel_id=1, source_target_pairs={{0,16},{4,20},{8,24},{12,28},{16,0},{20,4},{24,8},{28,12},{32,48},... | collective-permute-start | bytes 49160 | tf_op jit(solution)/shard_map/ppermute | solution.py:111
  303.2 3.9 collective-permute-start.14
  307.1 5.6 %collective-permute-start.15 = (f32[64,64]{1,0:T(8,128)S(1)}, f32[64,64]{1,0:T(8,128)S(1)}, u32[]{:S(2)}, u32[]{:S(2)}) collective-permute-start(f32[64,64]{1,0:T(8,128)S(1)} %add.918), channel_id=1, source_target_pairs={{0,64},{4,68},{8,72},{12,76},{16,80},{20,84},{24,88},{28,92},{32,9... | collective-permute-start | bytes 49160 | tf_op jit(solution)/shard_map/ppermute | solution.py:111
  312.7 3.9 collective-permute-start.16
  316.7 5.7 %collective-permute-start.17 = (f32[64,64]{1,0:T(8,128)S(1)}, f32[64,64]{1,0:T(8,128)S(1)}, u32[]{:S(2)}, u32[]{:S(2)}) collective-permute-start(f32[64,64]{1,0:T(8,128)S(1)} %add.920), channel_id=1, source_target_pairs={{0,2},{1,3},{2,0},{3,1},{4,6},{5,7},{6,4},{7,5},{8,10},{9,11},{10,... | collective-permute-start | bytes 49160 | tf_op jit(solution)/shard_map/ppermute | solution.py:111
  331.1 3.1 copy-start.2
  339.7 5.1 %slice-start = ((f32[64,192]{1,0:T(8,128)}), f32[64,128]{1,0:T(8,128)S(1)}, s32[]{:S(2)}) async-start(f32[64,192]{1,0:T(8,128)} %shard_map.41), calls=%async_computation.2 | async-start | bytes 65536 | tf_op jit(solution)/shard_map/concatenate | solution.py:164
  339.7 5.1 %copy-start.6 = (f32[64,128]{1,0:T(8,128)S(1)}, f32[64,128]{1,0:T(8,128)}, u32[]{:S(2)}) copy-start(f32[64,128]{1,0:T(8,128)} %shard_map.42) | copy-start | bytes 98308
  339.7 53.4 %all-to-all-start.1 = ((f32[128,1,72,128]{3,2,1,0:T(8,128)}), f32[128,1,72,128]{3,2,1,0:T(8,128)}, u32[]{:S(2)}, u32[]{:S(2)}) async-start(f32[128,1,72,128]{3,2,1,0:T(8,128)} %copy.12), calls=%async_computation.1 | async-start | bytes 9437184 | tf_op jit(solution)/shard_map/all_to_all | solution.py:186

commit v4 on v3

--- a/solution.py
+++ b/solution.py
@@ -1,3 +1,5 @@
+import functools
+
 import jax
 import jax.numpy as jnp
 from jax import lax
@@ -47,28 +49,58 @@
     return -2.0 * total + potential[None] * orbital_field
 
 
-def slab_terms(orbital_field, before, after):
-    width = before.shape[1]
-    planes = (
-        [before[:, q] for q in range(width)]
-        + [orbital_field[:, q] for q in range(orbital_field.shape[1])]
-        + [after[:, q] for q in range(width)]
-    )
-    rows = []
-    for p in range(orbital_field.shape[1]):
-        centre_plane = width + p
-        acc = coefs[1] * (planes[centre_plane + 1] + planes[centre_plane - 1])
+def combine_kernel(scale, with_base, *refs):
+    if with_base:
+        local_ref, own_ref, before_ref, after_ref, base_ref, out_ref = refs
+    else:
+        local_ref, own_ref, before_ref, after_ref, out_ref = refs
+    width = before_ref.shape[1]
+    planes_own = own_ref.shape[1]
+
+    def plane(q):
+        if q < 0:
+            return before_ref[:, width + q]
+        if q >= planes_own:
+            return after_ref[:, q - planes_own]
+        return own_ref[:, q]
+
+    for p in range(planes_own):
+        acc = coefs[1] * (plane(p + 1) + plane(p - 1))
         for k in range(2, 7):
-            acc = acc + coefs[k] * (planes[centre_plane + k] + planes[centre_plane - k])
-        rows.append(acc)
-    return jnp.stack(rows, axis=1)
-
-
-def hamiltonian(orbital_field, potential):
+            acc = acc + coefs[k] * (plane(p + k) + plane(p - k))
+        value = local_ref[:, p] - 2.0 * acc
+        value = scale * (value - centre * own_ref[:, p]) / radius
+        if with_base:
+            value = value - base_ref[:, p]
+        out_ref[:, p] = value
+
+
+def filter_step(local, orbital_field, before, after, scale, base=None):
+    rows = orbital_field.shape[0]
+    block_rows = 4 if rows % 4 == 0 else 1
+    block = (block_rows,) + orbital_field.shape[1:]
+    halo_block = (block_rows,) + before.shape[1:]
+    spec = pl.BlockSpec(block, lambda i: (i, 0, 0, 0))
+    halo_spec = pl.BlockSpec(halo_block, lambda i: (i, 0, 0, 0))
+    operands = [local, orbital_field, before, after]
+    specs = [spec, spec, halo_spec, halo_spec]
+    if base is not None:
+        operands.append(base)
+        specs.append(spec)
+    return pl.pallas_call(
+        functools.partial(combine_kernel, scale, base is not None),
+        grid=(rows // block_rows,),
+        in_specs=specs,
+        out_specs=spec,
+        out_shape=jax.ShapeDtypeStruct(orbital_field.shape, jnp.float32),
+    )(*operands)
+
+
+def chebyshev_step(orbital_field, potential, scale, base=None):
     before, after = halo_planes(orbital_field, "grid", 6)
     local = local_terms(orbital_field, potential)
     local, before, after = lax.optimization_barrier((local, before, after))
-    return local - 2.0 * slab_terms(orbital_field, before, after)
+    return filter_step(local, orbital_field, before, after, scale, base)
 
 
 def gram_matrix(left_rows, right_rows):
@@ -101,15 +133,37 @@
     )
 
 
+def group_round(value, axis, stride, radix):
+    size = lax.axis_size(axis)
+    position = (lax.axis_index(axis) // stride) % radix
+    received = [value]
+    for shift in range(1, radix):
+        pairs = []
+        for i in range(size):
+            p = (i // stride) % radix
+            pairs.append((i, i + ((p + shift) % radix - p) * stride))
+        received.append(lax.ppermute(value, axis, pairs))
+    total = None
+    for q in range(radix):
+        choice = (position - q) % radix
+        term = received[0]
+        for shift in range(1, radix):
+            term = jnp.where(choice == shift, received[shift], term)
+        total = term if total is None else total + term
+    return total
+
+
 def exchange_sum(value, axis):
     size = lax.axis_size(axis)
     if size & (size - 1):
         return lax.psum(value, axis)
-    step = 1
-    while step < size:
-        pairs = [(i, i ^ step) for i in range(size)]
-        value = value + lax.ppermute(value, axis, pairs)
-        step *= 2
+    stride = 1
+    if size.bit_length() % 2 == 0:
+        value = group_round(value, axis, 1, 2)
+        stride = 2
+    while stride < size:
+        value = group_round(value, axis, stride, 4)
+        stride *= 4
     return value
 
 
@@ -171,8 +225,8 @@
 
 def local(orbital_block, potential):
     orb_rows = orbital_block.shape[0]
-    first = (hamiltonian(orbital_block, potential) - centre * orbital_block) / radius
-    filtered = 2.0 * (hamiltonian(first, potential) - centre * first) / radius - orbital_block
+    first = chebyshev_step(orbital_block, potential, 1.0)
+    filtered = chebyshev_step(first, potential, 2.0, orbital_block)
     parts = lax.axis_size("orb")
     lanes = orbital_block.shape[3]
     rows_per_part = orbital_block.shape[1] * orbital_block.shape[2] // parts

time: 406 us -> 358 us (0.88); the launches traced: 399 us -> 357 us
  starting transfers between devices: 101 us -> 41.5 us
  other arithmetic: 132 us -> 105 us
  Pallas kernels: 16.4 us -> 40.1 us
  blocking collectives: 35.9 us -> 59.2 us
  waiting for transfers between devices: 81.4 us -> 75.3 us
    ppermute x14 -> x20, starting transfers between devices: 82.7 us -> 24.1 us  [group_round(): received.append(lax.ppermute(value, axis, pairs))]
    unnamed x10 -> x0, other arithmetic: 36.7 us -> none
    add x2, other arithmetic: 69.7 us -> 102 us  [local_terms(): return -2.0 * total + potential[None] * orbital_field]
    pallas_call x0 -> x2, Pallas kernels: none -> 23.7 us  [filter_step(): pl.pallas_call(functools.partial(combine_kernel, scale, base is not None)...]
    all_to_all x1, blocking collectives: 35.9 us -> 59.2 us  [local(): lax.all_to_all(filtered, 'orb', 1, 0, tiled=True)]
    ppermute x14 -> x20, waiting for transfers between devices: 33.9 us -> 25 us  [group_round(): received.append(lax.ppermute(value, axis, pairs))]
    another operation x2 -> x0, other arithmetic: 7.99 us -> none  [slab_terms(): return jnp.stack(rows, axis=1)]
    div x1 -> x0, other arithmetic: 7.44 us -> none  [local(): (hamiltonian(orbital_block, potential) - centre * orbital_block) / radius]
  transfers between devices with their start and end apart: 19 -> 25, of which waited for: 15 -> 19; matrix products, arithmetic and copies ran while one was open for 18% -> 30% of each run, Pallas kernels for 0% -> 0%
where the time goes in v4:
time: 358 us; the launch traced here: 357 us
  other arithmetic  105 us (29%)
  waiting for transfers between devices  75.3 us (21%)
  blocking collectives  59.2 us (17%)
  starting transfers between devices  41.5 us (12%)
  Pallas kernels  40.1 us (11%)
  local copies, waits for them, and re-layouts  19.3 us (5%)
  matrix products  15.4 us (4%)
    add x2, other arithmetic, local_terms(): return -2.0 * total + potential[None] * orbital_field  102 us
    all_to_all x1, blocking collectives, local(): lax.all_to_all(filtered, 'orb', 1, 0, tiled=True)  59.2 us
    all_to_all x1, waiting for transfers between devices, local(): orbitals = lax.all_to_all(orbitals, 'orb', 0, 1, tiled=True)  50.3 us
    ppermute x20, waiting for transfers between devices, group_round(): received.append(lax.ppermute(value, axis, pairs))  25 us
    ppermute x20, starting transfers between devices, group_round(): received.append(lax.ppermute(value, axis, pairs))  24.1 us
    pallas_call x2, Pallas kernels, filter_step(): pl.pallas_call(functools.partial(combine_kernel, scale, base is not None)...  23.7 us
    pallas_call x2, Pallas kernels, eliminate(): pl.pallas_call(eliminate_kernel, out_shape=jax.ShapeDtypeStruct(source.sh...  16.4 us
    ppermute x2, starting transfers between devices, halo_planes(): before = lax.ppermute(last, axis, up)  9.7 us
  transfers between devices with their start and end apart: 25, of which 19 were waited for; matrix products, arithmetic and copies ran while one was open for 30% of the time, Pallas kernels for 0%

profile of v4, /device:TPU:0, one launch (start us, length us, event | category | flops | bytes accessed | tf_op | source)
XLA Modules:
  0.0 356.8 jit_solution(16105385544248549742)
XLA Ops:
  0.6 3.5 collective-permute-start
  5.4 52.5 %multiply_add_fusion.1.refs_0_ = f32[32,6,48,128]{3,2,1,0:T(8,128)} fusion(f32[32,6,48,128]{3,2,1,0:T(8,128)} %refs_4_.1, f32[6,48,128]{2,1,0:T(8,128)} %param.3), kind=kLoop, calls=%fused_computation.122 | loop fusion | flops 47185920 | bytes 9584640 | tf_op jit(solution)/shard_map/add | solution.py:49
  58.0 11.3 %shard_map.41.refs_1_ = f32[32,6,48,128]{3,2,1,0:T(8,128)} custom-call(f32[32,6,48,128]{3,2,1,0:T(8,128)} %multiply_add_fusion.1.refs_0_, f32[32,6,48,128]{3,2,1,0:T(8,128)} %refs_4_.1, f32[32,6,48,128]{3,2,1,0:T(8,128)} %collective-permute-done.refs_2_, f32[32,6,48,128]{3,2,1,0:T(8,128)} %collective-permute-done.1.refs_3_), custom_call_target="tpu_custom_call" | custom-call | tf_op jit(solution)/shard_map/pallas_call | solution.py:90
  69.3 6.2 %collective-permute-start.2 = (f32[32,6,48,128]{3,2,1,0:T(8,128)}, f32[32,6,48,128]{3,2,1,0:T(8,128)}, u32[]{:S(2)}, u32[]{:S(2)}) collective-permute-start(f32[32,6,48,128]{3,2,1,0:T(8,128)} %shard_map.41.refs_1_), channel_id=1, source_target_pairs={{0,4},{4,8},{8,12},{12,16},{16,20},{20,24},{24,28},{28,32},{32,36}... | collective-permute-start | bytes 14155784 | tf_op jit(solution)/shard_map/ppermute | solution.py:30
  76.8 49.8 %multiply_add_fusion.refs_0_ = f32[32,6,48,128]{3,2,1,0:T(8,128)} fusion(f32[32,6,48,128]{3,2,1,0:T(8,128)} %shard_map.41.refs_1_, f32[6,48,128]{2,1,0:T(8,128)S(1)} %copy-done.3), kind=kLoop, calls=%fused_computation.121 | loop fusion | flops 47185920 | bytes 9584640 | tf_op jit(solution)/shard_map/add | solution.py:49
  126.6 12.4 %shard_map.42 = f32[32,6,48,128]{3,2,1,0:T(8,128)} custom-call(f32[32,6,48,128]{3,2,1,0:T(8,128)} %multiply_add_fusion.refs_0_, f32[32,6,48,128]{3,2,1,0:T(8,128)} %shard_map.41.refs_1_, f32[32,6,48,128]{3,2,1,0:T(8,128)} %collective-permute-done.2.refs_2_, f32[32,6,48,128]{3,2,1,0:T(8,128)} %collective-permute-done.3.refs_3_, f32[32,6,48,128]{3,2,1,0:T(8,128)} %refs_4_.1), custom_call_target="tpu_custom_call" | custom-call | tf_op jit(solution)/shard_map/pallas_call | solution.py:90
  138.9 2.6 copy.9
  141.6 59.2 %all_to_all.30 = f32[32,4,72,128]{3,2,0,1:T(8,128)S(1)} all-to-all(f32[32,4,72,128]{3,2,0,1:T(8,128)S(1)} %copy.9), channel_id=1, replica_groups=mesh['grid'=32,'orb'=4] {'orb'}, dimensions={1} | all-to-all | bytes 9437184 | tf_op jit(solution)/shard_map/all_to_all | solution.py:235
  200.8 1.7 fusion.75
  203.9 5.0 %convolution_bitcast_fusion.1 = f32[64,128]{1,0:T(8,128)S(1)} fusion(f32[64,72,128]{2,0,1:T(8,128)S(1)} %bitcast.36, f32[128,72,128]{2,0,1:T(8,128)S(1)} %bitcast.39), kind=kOutput, calls=%fused_computation.125 | convolution fusion | flops 905969664 | bytes 7110656 | tf_op jit(solution)/shard_map/dot_general | solution.py:107
  208.9 1.6 collective-permute-start.4
  211.4 5.3 %collective-permute-start.5 = (f32[64,128]{1,0:T(8,128)S(1)}, f32[64,128]{1,0:T(8,128)S(1)}, u32[]{:S(2)}, u32[]{:S(2)}) collective-permute-start(f32[64,128]{1,0:T(8,128)S(1)} %select_add_fusion.5), channel_id=1, source_target_pairs={{0,24},{4,28},{8,0},{12,4},{16,8},{20,12},{24,16},{28,20},{32,56},... | collective-permute-start | bytes 98312 | tf_op jit(solution)/shard_map/ppermute | solution.py:145
  218.3 3.8 %collective-permute-done.6 = f32[64,128]{1,0:T(8,128)S(1)} collective-permute-done((f32[64,128]{1,0:T(8,128)S(1)}, f32[64,128]{1,0:T(8,128)S(1)}, u32[]{:S(2)}, u32[]{:S(2)}) %collective-permute-start.6) | collective-permute-done | bytes 32800 | tf_op jit(solution)/shard_map/ppermute | solution.py:145
  222.2 2.0 collective-permute-start.8
  224.2 1.6 collective-permute-start.9
  226.4 3.2 collective-permute-done.9
  233.8 3.5 copy.12
  239.4 8.4 %shard_map.43 = f32[64,192]{1,0:T(8,128)} custom-call(f32[64,192]{1,0:T(8,128)} %pad_maximum_fusion.source_ref), custom_call_target="tpu_custom_call" | custom-call | tf_op jit(solution)/shard_map/pallas_call | solution.py:198
  247.8 3.1 fusion.73
  251.0 2.3 convolution_subtract_fusion
  253.3 2.0 convolution_bitcast_fusion
  260.7 2.3 collective-permute-done.16
  266.1 1.7 collective-permute-done.18
  267.8 1.7 collective-permute-done.19
  270.5 1.7 collective-permute-start.21
  274.5 3.2 collective-permute-done.22
  279.0 8.0 %shard_map.44 = f32[64,128]{1,0:T(8,128)} custom-call(f32[64,128]{1,0:T(8,128)} %pad_maximum_fusion.1.source_ref), custom_call_target="tpu_custom_call" | custom-call | tf_op jit(solution)/shard_map/pallas_call | solution.py:198
  287.0 3.1 fusion.72
  290.6 4.9 %copy.14 = f32[128,1,72,128]{3,2,1,0:T(8,128)} copy(f32[128,1,72,128]{3,0,2,1:T(8,128)S(1)} %maximum_bitcast_fusion) | data formatting | bytes 9437184 | tf_op jit(solution)/shard_map/reshape | solution.py:239
  295.6 5.1 %all-to-all-start.1 = ((f32[128,1,72,128]{3,2,1,0:T(8,128)}), f32[128,1,72,128]{3,2,1,0:T(8,128)}, u32[]{:S(2)}, u32[]{:S(2)}) async-start(f32[128,1,72,128]{3,2,1,0:T(8,128)} %copy.14), calls=%async_computation.1 | async-start | bytes 9437184 | tf_op jit(solution)/shard_map/all_to_all | solution.py:240
  301.4 50.3 %all-to-all-done.1 = f32[128,1,72,128]{3,2,1,0:T(8,128)} async-done(((f32[128,1,72,128]{3,2,1,0:T(8,128)}), f32[128,1,72,128]{3,2,1,0:T(8,128)}, u32[]{:S(2)}, u32[]{:S(2)}) %all-to-all-start.1) | async-done | bytes 4718624 | tf_op jit(solution)/shard_map/all_to_all | solution.py:240
  351.7 5.1 %copy.15 = f32[32,4,1,72,128]{4,3,1,0,2:T(8,128)} copy(f32[32,4,1,72,128]{4,3,0,1,2:T(8,128)} %bitcast.14) | data formatting | bytes 9437184 | tf_op jit(solution)/shard_map/all_to_all | solution.py:240
  (64 shorter events, 27.7 us)
Async XLA Ops:
  0.6 57.3 %collective-permute-start = (f32[32,6,48,128]{3,2,1,0:T(8,128)}, f32[32,6,48,128]{3,2,1,0:T(8,128)}, u32[]{:S(2)}, u32[]{:S(2)}) collective-permute-start(f32[32,6,48,128]{3,2,1,0:T(8,128)} %refs_4_.1), channel_id=1, source_target_pairs={{0,4},{4,8},{8,12},{12,16},{16,20},{20,24},{24,28},{28,32},{32,36}... | collective-permute-start | bytes 14155784 | tf_op jit(solution)/shard_map/ppermute | solution.py:30
  4.1 53.8 %collective-permute-start.1 = (f32[32,6,48,128]{3,2,1,0:T(8,128)}, f32[32,6,48,128]{3,2,1,0:T(8,128)}, u32[]{:S(2)}, u32[]{:S(2)}) collective-permute-start(f32[32,6,48,128]{3,2,1,0:T(8,128)} %refs_4_.1), channel_id=1, source_target_pairs={{4,0},{8,4},{12,8},{16,12},{20,16},{24,20},{28,24},{32,28},{36,32}... | collective-permute-start | bytes 14155784 | tf_op jit(solution)/shard_map/ppermute | solution.py:31
  57.9 18.8 %copy-start.3 = (f32[6,48,128]{2,1,0:T(8,128)S(1)}, f32[6,48,128]{2,1,0:T(8,128)}, u32[]{:S(2)}) copy-start(f32[6,48,128]{2,1,0:T(8,128)} %param.3) | copy-start | bytes 442372
  69.3 57.3 %collective-permute-start.2 = (f32[32,6,48,128]{3,2,1,0:T(8,128)}, f32[32,6,48,128]{3,2,1,0:T(8,128)}, u32[]{:S(2)}, u32[]{:S(2)}) collective-permute-start(f32[32,6,48,128]{3,2,1,0:T(8,128)} %shard_map.41.refs_1_), channel_id=1, source_target_pairs={{0,4},{4,8},{8,12},{12,16},{16,20},{20,24},{24,28},{28,32},{32,36}... | collective-permute-start | bytes 14155784 | tf_op jit(solution)/shard_map/ppermute | solution.py:30
  75.5 51.1 %collective-permute-start.3 = (f32[32,6,48,128]{3,2,1,0:T(8,128)}, f32[32,6,48,128]{3,2,1,0:T(8,128)}, u32[]{:S(2)}, u32[]{:S(2)}) collective-permute-start(f32[32,6,48,128]{3,2,1,0:T(8,128)} %shard_map.41.refs_1_), channel_id=1, source_target_pairs={{4,0},{8,4},{12,8},{16,12},{20,16},{24,20},{28,24},{32,28},{36,32}... | collective-permute-start | bytes 14155784 | tf_op jit(solution)/shard_map/ppermute | solution.py:31
  208.9 2.5 collective-permute-start.4
  211.4 6.9 %collective-permute-start.5 = (f32[64,128]{1,0:T(8,128)S(1)}, f32[64,128]{1,0:T(8,128)S(1)}, u32[]{:S(2)}, u32[]{:S(2)}) collective-permute-start(f32[64,128]{1,0:T(8,128)S(1)} %select_add_fusion.5), channel_id=1, source_target_pairs={{0,24},{4,28},{8,0},{12,4},{16,8},{20,12},{24,16},{28,20},{32,56},... | collective-permute-start | bytes 98312 | tf_op jit(solution)/shard_map/ppermute | solution.py:145
  216.7 5.4 %collective-permute-start.6 = (f32[64,128]{1,0:T(8,128)S(1)}, f32[64,128]{1,0:T(8,128)S(1)}, u32[]{:S(2)}, u32[]{:S(2)}) collective-permute-start(f32[64,128]{1,0:T(8,128)S(1)} %select_add_fusion.5), channel_id=1, source_target_pairs={{0,16},{4,20},{8,24},{12,28},{16,0},{20,4},{24,8},{28,12},{32,48},... | collective-permute-start | bytes 98312 | tf_op jit(solution)/shard_map/ppermute | solution.py:145
  216.7 5.5 %collective-permute-start.7 = (f32[64,128]{1,0:T(8,128)S(1)}, f32[64,128]{1,0:T(8,128)S(1)}, u32[]{:S(2)}, u32[]{:S(2)}) collective-permute-start(f32[64,128]{1,0:T(8,128)S(1)} %select_add_fusion.5), channel_id=1, source_target_pairs={{0,8},{4,12},{8,16},{12,20},{16,24},{20,28},{24,0},{28,4},{32,40},... | collective-permute-start | bytes 98312 | tf_op jit(solution)/shard_map/ppermute | solution.py:145
  222.2 4.2 %collective-permute-start.8 = (f32[64,128]{1,0:T(8,128)S(1)}, f32[64,128]{1,0:T(8,128)S(1)}, u32[]{:S(2)}, u32[]{:S(2)}) collective-permute-start(f32[64,128]{1,0:T(8,128)S(1)} %select_add_fusion.4), channel_id=1, source_target_pairs={{0,96},{4,100},{8,104},{12,108},{16,112},{20,116},{24,120},{28,124... | collective-permute-start | bytes 98312 | tf_op jit(solution)/shard_map/ppermute | solution.py:145
  224.2 5.4 %collective-permute-start.9 = (f32[64,128]{1,0:T(8,128)S(1)}, f32[64,128]{1,0:T(8,128)S(1)}, u32[]{:S(2)}, u32[]{:S(2)}) collective-permute-start(f32[64,128]{1,0:T(8,128)S(1)} %select_add_fusion.4), channel_id=1, source_target_pairs={{0,64},{4,68},{8,72},{12,76},{16,80},{20,84},{24,88},{28,92},{32,9... | collective-permute-start | bytes 98312 | tf_op jit(solution)/shard_map/ppermute | solution.py:145
  225.8 5.1 %collective-permute-start.10 = (f32[64,128]{1,0:T(8,128)S(1)}, f32[64,128]{1,0:T(8,128)S(1)}, u32[]{:S(2)}, u32[]{:S(2)}) collective-permute-start(f32[64,128]{1,0:T(8,128)S(1)} %select_add_fusion.4), channel_id=1, source_target_pairs={{0,32},{4,36},{8,40},{12,44},{16,48},{20,52},{24,56},{28,60},{32,6... | collective-permute-start | bytes 98312 | tf_op jit(solution)/shard_map/ppermute | solution.py:145
  231.0 6.4 %collective-permute-start.11 = (f32[64,128]{1,0:T(8,128)S(1)}, f32[64,128]{1,0:T(8,128)S(1)}, u32[]{:S(2)}, u32[]{:S(2)}) collective-permute-start(f32[64,128]{1,0:T(8,128)S(1)} %select_add_fusion.3), channel_id=1, source_target_pairs={{0,3},{1,0},{2,1},{3,2},{4,7},{5,4},{6,5},{7,6},{8,11},{9,8},{10,9... | collective-permute-start | bytes 98312 | tf_op jit(solution)/shard_map/ppermute | solution.py:145
  232.2 5.4 %collective-permute-start.12 = (f32[64,128]{1,0:T(8,128)S(1)}, f32[64,128]{1,0:T(8,128)S(1)}, u32[]{:S(2)}, u32[]{:S(2)}) collective-permute-start(f32[64,128]{1,0:T(8,128)S(1)} %select_add_fusion.3), channel_id=1, source_target_pairs={{0,2},{1,3},{2,0},{3,1},{4,6},{5,7},{6,4},{7,5},{8,10},{9,11},{10,... | collective-permute-start | bytes 98312 | tf_op jit(solution)/shard_map/ppermute | solution.py:145
  233.7 5.1 %collective-permute-start.13 = (f32[64,128]{1,0:T(8,128)S(1)}, f32[64,128]{1,0:T(8,128)S(1)}, u32[]{:S(2)}, u32[]{:S(2)}) collective-permute-start(f32[64,128]{1,0:T(8,128)S(1)} %select_add_fusion.3), channel_id=1, source_target_pairs={{0,1},{1,2},{2,3},{3,0},{4,5},{5,6},{6,7},{7,4},{8,9},{9,10},{10,1... | collective-permute-start | bytes 98312 | tf_op jit(solution)/shard_map/ppermute | solution.py:145
  247.8 3.1 copy-start.2
  247.8 3.1 copy-start.4
  250.9 4.3 %copy-start = (f32[64,72,128]{2,0,1:T(8,128)}, f32[64,72,128]{2,0,1:T(8,128)S(1)}, u32[]{:S(2)}) copy-start(f32[64,72,128]{2,0,1:T(8,128)S(1)} %fusion.73) | copy-start | bytes 7077892
  255.2 1.3 collective-permute-start.14
  256.5 4.1 %collective-permute-start.15 = (f32[64,64]{1,0:T(8,128)S(1)}, f32[64,64]{1,0:T(8,128)S(1)}, u32[]{:S(2)}, u32[]{:S(2)}) collective-permute-start(f32[64,64]{1,0:T(8,128)S(1)} %select_add_fusion.2), channel_id=1, source_target_pairs={{0,24},{4,28},{8,0},{12,4},{16,8},{20,12},{24,16},{28,20},{32,56},... | collective-permute-start | bytes 49160 | tf_op jit(solution)/shard_map/ppermute | solution.py:145
  257.5 5.5 %collective-permute-start.16 = (f32[64,64]{1,0:T(8,128)S(1)}, f32[64,64]{1,0:T(8,128)S(1)}, u32[]{:S(2)}, u32[]{:S(2)}) collective-permute-start(f32[64,64]{1,0:T(8,128)S(1)} %select_add_fusion.2), channel_id=1, source_target_pairs={{0,16},{4,20},{8,24},{12,28},{16,0},{20,4},{24,8},{28,12},{32,48},... | collective-permute-start | bytes 49160 | tf_op jit(solution)/shard_map/ppermute | solution.py:145
  258.7 5.1 %collective-permute-start.17 = (f32[64,64]{1,0:T(8,128)S(1)}, f32[64,64]{1,0:T(8,128)S(1)}, u32[]{:S(2)}, u32[]{:S(2)}) collective-permute-start(f32[64,64]{1,0:T(8,128)S(1)} %select_add_fusion.2), channel_id=1, source_target_pairs={{0,8},{4,12},{8,16},{12,20},{16,24},{20,28},{24,0},{28,4},{32,40},... | collective-permute-start | bytes 49160 | tf_op jit(solution)/shard_map/ppermute | solution.py:145
  263.8 4.0 %collective-permute-start.18 = (f32[64,64]{1,0:T(8,128)S(1)}, f32[64,64]{1,0:T(8,128)S(1)}, u32[]{:S(2)}, u32[]{:S(2)}) collective-permute-start(f32[64,64]{1,0:T(8,128)S(1)} %select_add_fusion.1), channel_id=1, source_target_pairs={{0,96},{4,100},{8,104},{12,108},{16,112},{20,116},{24,120},{28,124... | collective-permute-start | bytes 49160 | tf_op jit(solution)/shard_map/ppermute | solution.py:145
  263.9 5.6 %collective-permute-start.19 = (f32[64,64]{1,0:T(8,128)S(1)}, f32[64,64]{1,0:T(8,128)S(1)}, u32[]{:S(2)}, u32[]{:S(2)}) collective-permute-start(f32[64,64]{1,0:T(8,128)S(1)} %select_add_fusion.1), channel_id=1, source_target_pairs={{0,64},{4,68},{8,72},{12,76},{16,80},{20,84},{24,88},{28,92},{32,9... | collective-permute-start | bytes 49160 | tf_op jit(solution)/shard_map/ppermute | solution.py:145
  265.3 5.1 %collective-permute-start.20 = (f32[64,64]{1,0:T(8,128)S(1)}, f32[64,64]{1,0:T(8,128)S(1)}, u32[]{:S(2)}, u32[]{:S(2)}) collective-permute-start(f32[64,64]{1,0:T(8,128)S(1)} %select_add_fusion.1), channel_id=1, source_target_pairs={{0,32},{4,36},{8,40},{12,44},{16,48},{20,52},{24,56},{28,60},{32,6... | collective-permute-start | bytes 49160 | tf_op jit(solution)/shard_map/ppermute | solution.py:145
  270.5 4.0 %collective-permute-start.21 = (f32[64,64]{1,0:T(8,128)S(1)}, f32[64,64]{1,0:T(8,128)S(1)}, u32[]{:S(2)}, u32[]{:S(2)}) collective-permute-start(f32[64,64]{1,0:T(8,128)S(1)} %select_add_fusion), channel_id=1, source_target_pairs={{0,3},{1,0},{2,1},{3,2},{4,7},{5,4},{6,5},{7,6},{8,11},{9,8},{10,9... | collective-permute-start | bytes 49160 | tf_op jit(solution)/shard_map/ppermute | solution.py:145
  272.3 5.4 %collective-permute-start.22 = (f32[64,64]{1,0:T(8,128)S(1)}, f32[64,64]{1,0:T(8,128)S(1)}, u32[]{:S(2)}, u32[]{:S(2)}) collective-permute-start(f32[64,64]{1,0:T(8,128)S(1)} %select_add_fusion), channel_id=1, source_target_pairs={{0,2},{1,3},{2,0},{3,1},{4,6},{5,7},{6,4},{7,5},{8,10},{9,11},{10,... | collective-permute-start | bytes 49160 | tf_op jit(solution)/shard_map/ppermute | solution.py:145
  273.1 5.1 %collective-permute-start.23 = (f32[64,64]{1,0:T(8,128)S(1)}, f32[64,64]{1,0:T(8,128)S(1)}, u32[]{:S(2)}, u32[]{:S(2)}) collective-permute-start(f32[64,64]{1,0:T(8,128)S(1)} %select_add_fusion), channel_id=1, source_target_pairs={{0,1},{1,2},{2,3},{3,0},{4,5},{5,6},{6,7},{7,4},{8,9},{9,10},{10,1... | collective-permute-start | bytes 49160 | tf_op jit(solution)/shard_map/ppermute | solution.py:145
  287.0 3.1 copy-start.1
  295.6 5.1 %slice-start = ((f32[64,192]{1,0:T(8,128)}), f32[64,128]{1,0:T(8,128)S(1)}, s32[]{:S(2)}) async-start(f32[64,192]{1,0:T(8,128)} %shard_map.43), calls=%async_computation.2 | async-start | bytes 65536 | tf_op jit(solution)/shard_map/concatenate | solution.py:218
  295.6 5.1 %copy-start.5 = (f32[64,128]{1,0:T(8,128)S(1)}, f32[64,128]{1,0:T(8,128)}, u32[]{:S(2)}) copy-start(f32[64,128]{1,0:T(8,128)} %shard_map.44) | copy-start | bytes 98308
  295.6 56.2 %all-to-all-start.1 = ((f32[128,1,72,128]{3,2,1,0:T(8,128)}), f32[128,1,72,128]{3,2,1,0:T(8,128)}, u32[]{:S(2)}, u32[]{:S(2)}) async-start(f32[128,1,72,128]{3,2,1,0:T(8,128)} %copy.14), calls=%async_computation.1 | async-start | bytes 9437184 | tf_op jit(solution)/shard_map/all_to_all | solution.py:240
